TPU v7x, 512 devices: a whole 4x4x16 slice. The times are simulated.
512 devices in a mesh: seq: 32 (over x, y, core), mp: 16 (over z).
Axes of the slice: x: 4, y: 4, z: 16, core: 2. Of those that a mesh axis runs over, the one named last changes fastest.
Arguments:
- token_ids: int32 [256, 4], replicated, may hold values from 0 to 151935
- embedding: bfloat16 [151936, 1536], P('seq', 'mp'), may hold values from -13 to 13
- attn_gain: float32 [1536], P('mp'), may hold values from 0.25 to 1.75
- w_qkv: bfloat16 [1536, 2048], P('mp', 'seq'), may hold values from -0.15625 to 0.15625
- w_out: bfloat16 [1536, 1536], P('seq', 'mp'), may hold values from -0.15625 to 0.15625
- prompt_cache: bfloat16 [2, 32, 2048, 256], P(None, 'mp', 'seq'), may hold values from -170 to 170
- request_cache: bfloat16 [2, 256, 2048, 256], P(None, 'mp', 'seq'), may hold values from -170 to 170
- group_ids: int32 [256], P('mp'), may hold values from 0 to 1
- prefix_len: int32 [32], P('mp'), may hold values from 1 to 2048
- suffix_len: int32 [256], P('mp'), may hold values from 0 to 2048
- moe_gain: float32 [1536], replicated, may hold values from 0.25 to 1.75
- w_router: bfloat16 [1536, 32], replicated, may hold values from -0.15625 to 0.15625
- w_gate_up: bfloat16 [32, 2, 768, 1536], P('seq', None, 'mp'), may hold values from -0.15625 to 0.15625
- w_down: bfloat16 [32, 768, 1536], P('seq', 'mp'), may hold values from -0.21875 to 0.21875
- routes: int32 [256, 4, 4], replicated, may hold values from 0 to 31, all different within a row; in each aligned block of 32 rows (0 to 31, 32 to 63, ..., all dimensions but the last counted through in order) at most 8 rows name the same one
Outputs:
- hidden_out: bfloat16 [256, 4, 1536], P('seq', None, 'mp')
Inputs may be any that keep to these rules, and one draw needn't show every extreme that they name: `routes`: in each aligned block of 32 rows (request, step) taken in order, the requests of one index of seq, no expert is named more than 8 times.
All inputs are finite; a program needn't handle non-finite values.
Results may differ from a plain program's by a relative error of at most 0.015.
The roundings to bfloat16 on the way count: a program that leaves them out, or rounds other values in their place, can miss the bound.
Values may be sent and summed in bfloat16 or wider, within the bound.
No kernel may reach another device: no remote copies, remote signals or barrier semaphores. Data moves between devices by JAX's collectives and lax.ppermute only.
A program may use at most 128 MiB of HBM per device.

v0:
```python
import math

import jax
import jax.numpy as jnp
from jax import lax
from jax.sharding import PartitionSpec as P

D = 1536
QUERY_HEADS = 12
KEY_VALUE_HEADS = 2
HEAD_SIZE = 128
E = 32
TOPK = 4
NEW_TOKENS = 4


EPS = 1e-06
NEG = -1e30


def rounded_float(values):
    return lax.optimization_barrier(values.astype(jnp.bfloat16)).astype(jnp.float32)


def norm_full(values, gain_vec):
    floats = values.astype(jnp.float32)
    mean_sq = jnp.mean(floats * floats, axis=-1, keepdims=True)
    return (floats * lax.rsqrt(mean_sq + EPS) * gain_vec).astype(jnp.bfloat16)


def slot_table(route_rows, expert_ids, capacity):
    hit_mask = jnp.any(route_rows[:, :, :, None] == expert_ids[None, None, None, :], axis=2)
    hit_count = hit_mask.astype(jnp.int32)
    ahead_count = jnp.cumsum(hit_count, axis=1) - hit_count
    slot_ids = jnp.arange(capacity, dtype=jnp.int32)
    chosen = hit_mask[..., None] & (ahead_count[..., None] == slot_ids)
    return jnp.transpose(chosen, (2, 0, 3, 1)).astype(jnp.bfloat16)


def member_table(route_rows):
    experts_all = jnp.arange(E, dtype=jnp.int32)
    return jnp.any(route_rows[..., None] == experts_all, axis=-2).astype(jnp.bfloat16)


def expert_hidden(slot_rows, member, expert, gate_up, router, gain_vec):
    normed = norm_full(slot_rows, gain_vec)
    logits = jnp.dot(normed, router, preferred_element_type=jnp.float32)
    which = (jnp.arange(logits.shape[1], dtype=jnp.int32) == expert).astype(jnp.float32)
    member_f = member.astype(jnp.float32)
    own_flag = jnp.sum(member_f * which, axis=1)
    own_logit = jnp.sum(logits * which, axis=1)
    denominator = jnp.sum(jnp.exp(logits) * member_f, axis=1)
    share = own_flag * jnp.exp(own_logit) / (denominator + 1.0 - own_flag)
    half_width = gate_up.shape[1]
    both = lax.dot_general(
        normed,
        gate_up.reshape(2 * half_width, gate_up.shape[-1]),
        (((1,), (1,)), ((), ())),
        preferred_element_type=jnp.float32,
    )
    hidden = (jnp.maximum(both[:, :half_width], 0.0) * both[:, half_width:]).astype(jnp.bfloat16)
    return (hidden, share)


def expert_block(rows_in, member_in, local_experts, w_gate_up, w_down, w_router, moe_gain):
    hidden, share = expert_hidden(
        rows_in[0], member_in[0], local_experts[0], w_gate_up[0], w_router, moe_gain
    )
    hiddens = [hidden]
    shares = [share]
    hidden_all = jnp.stack(hiddens)
    partials = jnp.einsum("xnf,xfd->xnd", hidden_all, w_down, preferred_element_type=jnp.float32)
    reduced = lax.psum_scatter(
        partials.astype(jnp.bfloat16), "mp", scatter_dimension=2, tiled=True
    ).astype(jnp.float32)
    share_all = jnp.stack(shares)
    return (share_all[..., None] * rounded_float(reduced)).astype(jnp.bfloat16)


def on_device(
    token_ids,
    embedding,
    attn_gain,
    w_qkv,
    w_out,
    prompt_cache,
    request_cache,
    group_ids,
    prefix_len,
    suffix_len,
    moe_gain,
    w_router,
    w_gate_up,
    w_down,
    routes,
):
    seq_count = lax.axis_size("seq")
    seq_index = lax.axis_index("seq")
    vocab_rows = embedding.shape[0]
    local_ids = token_ids - seq_index * vocab_rows
    inside = (local_ids >= 0) & (local_ids < vocab_rows)
    looked = jnp.take(embedding, jnp.clip(local_ids, 0, vocab_rows - 1), axis=0)
    emb_terms = jnp.where(inside[..., None], looked, jnp.zeros_like(looked)).astype(jnp.float32)
    resid = lax.psum_scatter(emb_terms.astype(jnp.bfloat16), "seq", scatter_dimension=0, tiled=True)
    floats = resid.astype(jnp.float32)
    square_sum = lax.psum(jnp.sum(floats * floats, axis=-1), "mp")
    normed = (floats * lax.rsqrt(square_sum[..., None] / D + EPS) * attn_gain).astype(jnp.bfloat16)
    normed_all = lax.all_gather(normed, "seq", axis=0, tiled=True)
    flat_normed = normed_all.reshape(-1, normed_all.shape[-1])
    row_block = flat_normed
    qkv_part = lax.psum_scatter(
        jnp.dot(row_block, w_qkv, preferred_element_type=jnp.float32),
        "mp",
        scatter_dimension=0,
        tiled=True,
    )
    projected_rows = lax.all_gather(qkv_part.astype(jnp.bfloat16), "seq", axis=1, tiled=True)
    request_count = group_ids.shape[0]
    prompt_group_count = prefix_len.shape[0]
    prefix_rows = prompt_cache.shape[2]
    suffix_rows = request_cache.shape[2]
    requests_per_group = QUERY_HEADS // KEY_VALUE_HEADS
    head_feature_width = QUERY_HEADS * HEAD_SIZE
    key_value_width = KEY_VALUE_HEADS * HEAD_SIZE
    projected_rows = projected_rows.reshape(request_count, NEW_TOKENS, -1)
    query_matrix = projected_rows[:, :, :head_feature_width].reshape(
        request_count, NEW_TOKENS, KEY_VALUE_HEADS, requests_per_group, HEAD_SIZE
    )
    fresh_key_rows = projected_rows[
        :, :, head_feature_width : head_feature_width + key_value_width
    ].reshape(request_count, NEW_TOKENS, KEY_VALUE_HEADS, HEAD_SIZE)
    fresh_value_rows = projected_rows[:, :, head_feature_width + key_value_width :].reshape(
        request_count, NEW_TOKENS, KEY_VALUE_HEADS, HEAD_SIZE
    )
    prefix_keys = prompt_cache[0].reshape(
        prompt_group_count, prefix_rows, KEY_VALUE_HEADS, HEAD_SIZE
    )
    prefix_values = prompt_cache[1].reshape(
        prompt_group_count, prefix_rows, KEY_VALUE_HEADS, HEAD_SIZE
    )
    suffix_keys = request_cache[0].reshape(request_count, suffix_rows, KEY_VALUE_HEADS, HEAD_SIZE)
    suffix_values = request_cache[1].reshape(request_count, suffix_rows, KEY_VALUE_HEADS, HEAD_SIZE)
    score_scale = 1.0 / math.sqrt(HEAD_SIZE)
    prefix_scores = (
        jnp.einsum(
            "rtkgd,cpkd->rtkgcp", query_matrix, prefix_keys, preferred_element_type=jnp.float32
        )
        * score_scale
    )
    suffix_scores = (
        jnp.einsum(
            "rtkgd,rpkd->rtkgp", query_matrix, suffix_keys, preferred_element_type=jnp.float32
        )
        * score_scale
    )
    pre_pos = seq_index * prefix_rows + jnp.arange(prefix_rows, dtype=jnp.int32)
    pre_valid = (
        group_ids[:, None, None] == jnp.arange(prompt_group_count, dtype=jnp.int32)[None, :, None]
    ) & (pre_pos[None, None, :] < prefix_len[None, :, None])
    suf_pos = seq_index * suffix_rows + jnp.arange(suffix_rows, dtype=jnp.int32)
    suf_valid = suf_pos[None, :] < suffix_len[:, None]
    split_position = prompt_group_count * prefix_rows
    all_scores = jnp.concatenate(
        [
            prefix_scores.reshape(
                request_count, NEW_TOKENS, KEY_VALUE_HEADS, requests_per_group, split_position
            ),
            suffix_scores,
        ],
        axis=-1,
    )
    all_valid = jnp.concatenate(
        [pre_valid.reshape(request_count, split_position), suf_valid], axis=-1
    )[:, None, None, None, :]
    all_scores = jnp.where(all_valid, all_scores, NEG)
    block_max = jnp.max(all_scores, axis=-1)
    block_probs = jnp.where(all_valid, jnp.exp(all_scores - block_max[..., None]), 0.0)
    block_sum = jnp.sum(block_probs, axis=-1)
    rounded = block_probs.astype(jnp.bfloat16)
    pre_part = rounded[..., :split_position].reshape(
        request_count,
        NEW_TOKENS,
        KEY_VALUE_HEADS,
        requests_per_group,
        prompt_group_count,
        prefix_rows,
    )
    block_acc = jnp.einsum(
        "rtkgcp,cpkd->rtkgd", pre_part, prefix_values, preferred_element_type=jnp.float32
    )
    block_acc = block_acc + jnp.einsum(
        "rtkgp,rpkd->rtkgd",
        rounded[..., split_position:],
        suffix_values,
        preferred_element_type=jnp.float32,
    )
    head_cols = w_out.shape[0]
    merged_max = lax.pmax(block_max, "seq")
    rescale = jnp.exp(block_max - merged_max)
    merged_sum, merged_acc = lax.psum((block_sum * rescale, block_acc * rescale[..., None]), "seq")
    new_scores = (
        jnp.einsum(
            "rtkgd,rukd->rtkgu", query_matrix, fresh_key_rows, preferred_element_type=jnp.float32
        )
        * score_scale
    )
    causal = (jnp.arange(NEW_TOKENS)[:, None] >= jnp.arange(NEW_TOKENS)[None, :])[
        None, :, None, None, :
    ]
    new_scores = jnp.where(causal, new_scores, NEG)
    new_max = jnp.max(new_scores, axis=-1)
    new_probs = jnp.where(causal, jnp.exp(new_scores - new_max[..., None]), 0.0)
    new_sum = jnp.sum(new_probs, axis=-1)
    new_acc = jnp.einsum(
        "rtkgu,rukd->rtkgd",
        new_probs.astype(jnp.bfloat16),
        fresh_value_rows,
        preferred_element_type=jnp.float32,
    )
    overall = jnp.maximum(merged_max, new_max)
    cache_weight = jnp.exp(merged_max - overall)
    own_weight = jnp.exp(new_max - overall)
    denominator = merged_sum * cache_weight + new_sum * own_weight
    attended = (
        merged_acc * cache_weight[..., None] + new_acc * own_weight[..., None]
    ) / denominator[..., None]
    attended = attended.astype(jnp.bfloat16).reshape(request_count, NEW_TOKENS, head_feature_width)
    own_cols = lax.dynamic_slice_in_dim(attended, seq_index * head_cols, head_cols, 2)
    all_heads = lax.all_gather(own_cols, "mp", axis=0, tiled=True)
    flat_heads = all_heads.reshape(-1, head_cols)
    tok_rows = resid.shape[0]
    block_rows = tok_rows * NEW_TOKENS
    row_block = flat_heads
    out_part = lax.psum_scatter(
        jnp.dot(row_block, w_out, preferred_element_type=jnp.float32),
        "seq",
        scatter_dimension=0,
        tiled=True,
    )
    resid = (resid.astype(jnp.float32) + out_part.reshape(resid.shape)).astype(jnp.bfloat16)
    capacity = max(2, 2 * TOPK * block_rows // E)
    exp_local = w_down.shape[0]
    model_cols = resid.shape[-1]
    local_experts = seq_index * exp_local + jnp.arange(exp_local, dtype=jnp.int32)
    route_blocks = routes.reshape(seq_count, block_rows, TOPK)
    rows_seq = lax.all_gather(resid, "seq", axis=0, tiled=True)
    full_rows = lax.all_gather(rows_seq, "mp", axis=2, tiled=True)
    chosen = slot_table(route_blocks, local_experts, capacity)
    member_rows = member_table(route_blocks)
    picked = jnp.einsum(
        "xbmn,bnc->xbmc",
        chosen,
        full_rows.reshape(seq_count, block_rows, D),
        preferred_element_type=jnp.float32,
    ).astype(jnp.bfloat16)
    picked_member = jnp.einsum(
        "xbmn,bne->xbme", chosen, member_rows, preferred_element_type=jnp.float32
    ).astype(jnp.bfloat16)
    weighted = expert_block(
        picked.reshape(exp_local, -1, D),
        picked_member.reshape(exp_local, -1, E),
        local_experts,
        w_gate_up,
        w_down,
        w_router,
        moe_gain,
    )
    token_terms = jnp.einsum(
        "xbmn,xbmc->bnc",
        chosen,
        weighted.reshape(exp_local, seq_count, capacity, model_cols),
        preferred_element_type=jnp.float32,
    )
    moe_out = lax.psum_scatter(
        token_terms.reshape(-1, NEW_TOKENS, model_cols).astype(jnp.bfloat16),
        "seq",
        scatter_dimension=0,
        tiled=True,
    ).astype(jnp.float32)
    return (resid.astype(jnp.float32) + moe_out).astype(jnp.bfloat16)


def solution(mesh):
    in_specs = (
        P(),
        P("seq", "mp"),
        P("mp"),
        P("mp", "seq"),
        P("seq", "mp"),
        P(None, "mp", "seq", None),
        P(None, "mp", "seq", None),
        P("mp"),
        P("mp"),
        P("mp"),
        P(),
        P(),
        P("seq", None, "mp", None),
        P("seq", "mp", None),
        P(),
    )
    out_specs = P("seq", None, "mp")
    return jax.shard_map(
        on_device, mesh=mesh, in_specs=in_specs, out_specs=out_specs, check_vma=False
    )
```

profile of v0, /device:TPU:1, one launch (start us, length us, event | category | flops | bytes accessed | tf_op | source)
XLA Modules:
  0.0 1147.3 jit_solution(9252434510931173416)
XLA Ops:
  7.6 2.2 copy.181
  10.1 3.2 gather_fusion
  13.4 2.0 select_select_fusion
  19.3 134.5 %all-reduce.8.cloned.1.call-done = bf16[256,4,96]{2,1,0:T(4,128)(2,1)} async-done(((bf16[256,4,96]{2,1,0:T(4,128)(2,1)}), bf16[256,4,96]{2,1,0:T(4,128)(2,1)}) %all-reduce.8.cloned.1.call-update) | async-done | bytes 196624
  154.7 24.3 %psum.21 = f32[8,4]{1,0:T(8,128)S(1)} all-reduce(f32[8,4]{1,0:T(8,128)S(1)} %fusion.68), channel_id=1, replica_groups=mesh['seq'=32,'mp'=16] {'mp'}, use_global_device_ids=true, to_apply=%region_2.3 | all-reduce | flops 32 | bytes 256 | tf_op jit(solution)/shard_map/psum | solution.py:106
  179.8 32.7 %all_gather.15 = bf16[256,4,96]{2,1,0:T(4,128)(2,1)S(1)} all-gather(bf16[8,4,96]{2,1,0:T(4,128)(2,1)S(1)} %fusion.70), channel_id=1, replica_groups=mesh['seq'=32,'mp'=16] {'seq'}, dimensions={0}, use_global_device_ids=true | all-gather | bytes 202752 | tf_op jit(solution)/shard_map/all_gather | solution.py:108
  213.7 53.4 %reduce-scatter.6.cloned.1.call-done = f32[64,64]{1,0:T(8,128)} async-done(((f32[1024,64]{1,0:T(8,128)}), f32[64,64]{1,0:T(8,128)}) %reduce-scatter.6.cloned.1.call-update) | async-done | bytes 16400 | tf_op jit(solution)/shard_map/reduce_scatter | solution.py:111
  267.9 36.5 %all_gather.16 = bf16[64,2048]{0,1:T(8,128)(2,1)S(1)} all-gather(bf16[64,64]{0,1:T(8,128)(2,1)S(1)} %copy.182), channel_id=1, replica_groups=mesh['seq'=32,'mp'=16] {'seq'}, dimensions={1}, use_global_device_ids=true | all-gather | bytes 270336 | tf_op jit(solution)/shard_map/all_gather | solution.py:117
  307.9 120.9 %pmax.7 = f32[16,4,2,6]{0,1,3,2:T(4,128)S(1)} all-reduce(f32[16,4,2,6]{0,1,3,2:T(4,128)S(1)} %copy.197), channel_id=1, replica_groups=mesh['seq'=32,'mp'=16] {'seq'}, use_global_device_ids=true, to_apply=%region_5.6 | all-reduce | flops 768 | bytes 6144 | tf_op jit(solution)/shard_map/pmax | solution.py:198
  428.8 123.8 %psum.23 = f32[16,4,2,6]{0,1,3,2:T(4,128)S(1)} all-reduce(f32[16,4,2,6]{0,1,3,2:T(4,128)S(1)} %bitcast.157), channel_id=1, replica_groups=mesh['seq'=32,'mp'=16] {'seq'}, use_global_device_ids=true, to_apply=%region_9.10 | all-reduce | flops 768 | bytes 6144 | tf_op jit(solution)/shard_map/psum | solution.py:200
  552.6 1.3 fusion.80
  557.1 131.5 %all-reduce.6.cloned.1.call-done = f32[16,4,2,6,128]{4,0,3,1,2:T(8,128)} async-done(((f32[16,4,2,6,128]{4,0,3,1,2:T(8,128)}), f32[16,4,2,6,128]{4,0,3,1,2:T(8,128)}) %all-reduce.6.cloned.1.call-update) | async-done | bytes 393232 | tf_op jit(solution)/shard_map/psum | solution.py:200
  688.6 1.4 fusion.31
  690.3 24.7 %all_gather.17 = bf16[256,4,48]{2,0,1:T(8,128)(2,1)S(1)} all-gather(bf16[16,4,48]{2,0,1:T(8,128)(2,1)S(1)} %constant_dynamic-slice_fusion), channel_id=1, replica_groups=mesh['seq'=32,'mp'=16] {'mp'}, dimensions={0}, use_global_device_ids=true | all-gather | bytes 104448 | tf_op jit(solution)/shard_map/all_gather | solution.py:229
  716.3 101.5 %reduce-scatter.8.cloned.1.call-done = f32[32,96]{1,0:T(8,128)} async-done(((f32[1024,96]{1,0:T(8,128)}), f32[32,96]{1,0:T(8,128)}) %reduce-scatter.8.cloned.1.call-update) | async-done | bytes 12304 | tf_op jit(solution)/shard_map/reduce_scatter | solution.py:234
  818.6 26.6 %all_gather.18 = bf16[256,4,96]{2,1,0:T(4,128)(2,1)S(1)} all-gather(bf16[8,4,96]{2,1,0:T(4,128)(2,1)S(1)} %fusion.71), channel_id=1, replica_groups=mesh['seq'=32,'mp'=16] {'seq'}, dimensions={0}, use_global_device_ids=true | all-gather | bytes 202752 | tf_op jit(solution)/shard_map/all_gather | solution.py:246
  846.6 64.4 %all-gather.2.cloned.1.call-done = bf16[256,4,1536]{0,1,2:T(4,128)(2,1)} async-done(((bf16[256,4,96]{0,1,2:T(4,128)(2,1)}), bf16[256,4,1536]{0,1,2:T(4,128)(2,1)}) %all-gather.2.cloned.1.call-update) | async-done | bytes 3145744 | tf_op jit(solution)/shard_map/all_gather | solution.py:247
  911.0 5.9 copy.218
  917.0 2.4 reshape.284
  919.4 2.5 multiply_reduce_fusion
  924.1 3.5 copy.249
  931.0 64.1 %reduce-scatter.10.cloned.1.call-done = bf16[96,256]{1,0:T(8,128)(2,1)} async-done(((bf16[1536,256]{1,0:T(8,128)(2,1)}), bf16[96,256]{1,0:T(8,128)(2,1)}) %reduce-scatter.10.cloned.1.call-update) | async-done | bytes 49168
  997.2 142.0 %all-reduce.10.cloned.1.call-done = bf16[256,4,96]{2,1,0:T(4,128)(2,1)} async-done(((bf16[256,4,96]{2,1,0:T(4,128)(2,1)}), bf16[256,4,96]{2,1,0:T(4,128)(2,1)}) %all-reduce.10.cloned.1.call-update) | async-done | bytes 196624
  1139.2 1.3 add_convert_fusion
  (135 shorter events, 25.9 us)
Async XLA Ops:
  6.5 915.4 %copy-start = (bf16[1,2,48,1536]{3,2,1,0:T(8,128)(2,1)S(1)}, bf16[1,2,48,1536]{3,2,1,0:T(8,128)(2,1)}, u32[]{:S(2)}) copy-start(bf16[1,2,48,1536]{3,2,1,0:T(8,128)(2,1)} %param.27) | copy-start | bytes 884740
  6.5 147.3 %all-reduce.8.cloned.1.call-start = ((), (), s32[]{:S(2)}) async-start(), calls=%async_computation.8 | async-start | bytes 524288
  10.1 5.4 copy-start.4
  10.1 5.4 copy-start.1
  15.4 251.6 %reduce-scatter.6.cloned.1.call-start = ((), (), s32[]{:S(2)}) async-start(), calls=%async_computation.3 | async-start | bytes 557056 | tf_op jit(solution)/shard_map/reduce_scatter | solution.py:111
  15.6 0.7 copy-start.13
  15.6 0.8 copy-start.10
  15.7 163.3 %copy-start.11 = (f32[96]{0:T(128)S(1)}, f32[96]{0:T(128)}, u32[]{:S(2)}) copy-start(f32[96]{0:T(128)} %param.17) | copy-start | bytes 1156
  15.7 196.8 %copy-start.8 = (bf16[96,64]{0,1:T(8,128)(2,1)S(1)}, bf16[96,64]{0,1:T(8,128)(2,1)}, u32[]{:S(2)}) copy-start(bf16[96,64]{0,1:T(8,128)(2,1)} %param.18) | copy-start | bytes 36868
  15.8 197.7 %copy-start.12 = (s32[16]{0:T(128)S(1)}, s32[16]{0:T(128)}, u32[]{:S(2)}) copy-start(s32[16]{0:T(128)} %param.24) | copy-start | bytes 196
  213.5 475.0 %all-reduce.6.cloned.1.call-start = ((), (), s32[]{:S(2)}) async-start(), calls=%async_computation.4 | async-start | bytes 786432 | tf_op jit(solution)/shard_map/psum | solution.py:200
  554.3 0.8 copy-start.2
  556.4 261.4 %reduce-scatter.8.cloned.1.call-start = ((), (), s32[]{:S(2)}) async-start(), calls=%async_computation.5 | async-start | bytes 540672 | tf_op jit(solution)/shard_map/reduce_scatter | solution.py:234
  557.0 158.2 %copy-start.9 = (bf16[48,96]{1,0:T(8,128)(2,1)S(1)}, bf16[48,96]{1,0:T(8,128)(2,1)}, u32[]{:S(2)}) copy-start(bf16[48,96]{1,0:T(8,128)(2,1)} %param.19) | copy-start | bytes 27652
  690.2 155.8 %copy-start.6 = (s32[256,4,4]{0,2,1:T(4,128)S(1)}, s32[256,4,4]{0,2,1:T(4,128)}, u32[]{:S(2)}) copy-start(s32[256,4,4]{0,2,1:T(4,128)} %param.29) | copy-start | bytes 49156
  716.3 194.7 %all-gather.2.cloned.1.call-start = ((), (), s32[]{:S(2)}) async-start(), calls=%async_computation.6 | async-start | bytes 3342336 | tf_op jit(solution)/shard_map/all_gather | solution.py:247
  846.0 149.0 %reduce-scatter.10.cloned.1.call-start = ((), (), s32[]{:S(2)}) async-start(), calls=%async_computation.7 | async-start | bytes 835584
  919.4 2.5 copy-start.7
  921.9 0.9 copy-start.3
  928.6 1.9 copy-start.5
  928.6 210.6 %all-reduce.10.cloned.1.call-start = ((), (), s32[]{:S(2)}) async-start(), calls=%async_computation.9 | async-start | bytes 524288
Sparse Core Ops, SparseCore 0:
  15.6 138.2 all-reduce.7
  213.6 53.3 reduce-scatter.5
  556.6 131.9 all-reduce.5
  716.4 101.3 reduce-scatter.7
  846.2 64.8 all-gather.1
  928.8 66.2 reduce-scatter.9
  998.3 140.8 all-reduce.9
where the time goes:
time: 1150 us
  waiting for transfers between devices  692 us (60%)
  blocking collectives  389 us (34%)
  local copies, waits for them, and re-layouts  28.3 us (2%)
  between operations  14.7 us (1%)
  matrix products  11.9 us (1%)
    unnamed x10, waiting for transfers between devices  341 us
    psum x1, waiting for transfers between devices, on_device(): lax.psum((block_sum * rescale, block_acc * rescale[..., None]), 'seq')  132 us
    psum x1, blocking collectives, on_device(): lax.psum((block_sum * rescale, block_acc * rescale[..., None]), 'seq')  124 us
    pmax x1, blocking collectives, on_device(): merged_max = lax.pmax(block_max, 'seq')  121 us
    reduce_scatter x1, waiting for transfers between devices, on_device(): lax.psum_scatter(jnp.dot(row_block, w_out, preferred_element_type=jnp.flo...  102 us
    all_gather x1, waiting for transfers between devices, on_device(): full_rows = lax.all_gather(rows_seq, 'mp', axis=2, tiled=True)  64.4 us
    reduce_scatter x1, waiting for transfers between devices, on_device(): lax.psum_scatter(jnp.dot(row_block, w_qkv, preferred_element_type=jnp.flo...  53.4 us
    all_gather x1, blocking collectives, on_device(): lax.all_gather(qkv_part.astype(jnp.bfloat16), 'seq', axis=1, tiled=True)  36.5 us
  transfers between devices with their start and end apart: 7, of which 7 were waited for; matrix products, arithmetic and copies ran while one was open for 1% of the time, Pallas kernels for 0%

commit v1 on v0

v1 whole, which is shorter than its diff:
```python
import math

import numpy as np

import jax
import jax.numpy as jnp
from jax import lax
from jax.sharding import PartitionSpec as P

D = 1536
QUERY_HEADS = 12
KEY_VALUE_HEADS = 2
HEAD_SIZE = 128
E = 32
TOPK = 4
NEW_TOKENS = 4
MOST = 8

EPS = 1e-06
NEG = -1e30


def exchange(values, axis):
    return lax.all_to_all(values, axis, 0, 0, tiled=True)


def on_device(
    token_ids,
    embedding,
    attn_gain,
    w_qkv,
    w_out,
    prompt_cache,
    request_cache,
    group_ids,
    prefix_len,
    suffix_len,
    moe_gain,
    w_router,
    w_gate_up,
    w_down,
    routes,
):
    n_seq = lax.axis_size("seq")
    n_mp = lax.axis_size("mp")
    s = lax.axis_index("seq")
    total_rows = token_ids.shape[0] * NEW_TOKENS
    home_rows = total_rows // n_seq
    feat_mp = embedding.shape[1]

    vocab_rows = embedding.shape[0]
    local_ids = token_ids.reshape(total_rows) - s * vocab_rows
    inside = (local_ids >= 0) & (local_ids < vocab_rows)
    looked = jnp.take(embedding, jnp.clip(local_ids, 0, vocab_rows - 1), axis=0)
    looked = jnp.where(inside[:, None], looked, jnp.zeros_like(looked))
    got = exchange(looked.reshape(n_seq, home_rows, feat_mp), "seq")
    x_home = jnp.sum(got.astype(jnp.float32), axis=0)

    square_sum = lax.psum(jnp.sum(x_home * x_home, axis=-1), "mp")
    normed = (x_home * lax.rsqrt(square_sum[:, None] / D + EPS) * attn_gain).astype(jnp.bfloat16)
    normed_all = lax.all_gather(normed, "seq", axis=0, tiled=True)

    qkv_part = jnp.dot(normed_all, w_qkv, preferred_element_type=jnp.float32)
    attn_rows = total_rows // n_mp
    qkv_got = exchange(qkv_part.reshape(n_mp, attn_rows, qkv_part.shape[-1]), "mp")
    qkv_cols = jnp.sum(qkv_got, axis=0).astype(jnp.bfloat16)
    qkv_rows = lax.all_gather(qkv_cols, "seq", axis=1, tiled=True)

    request_count = group_ids.shape[0]
    groups_per = QUERY_HEADS // KEY_VALUE_HEADS
    qf = QUERY_HEADS * HEAD_SIZE
    kf = KEY_VALUE_HEADS * HEAD_SIZE
    q = qkv_rows[:, :qf].reshape(request_count, NEW_TOKENS, KEY_VALUE_HEADS, groups_per, HEAD_SIZE)
    k_new = qkv_rows[:, qf : qf + kf].reshape(request_count, NEW_TOKENS, KEY_VALUE_HEADS, HEAD_SIZE)
    v_new = qkv_rows[:, qf + kf :].reshape(request_count, NEW_TOKENS, KEY_VALUE_HEADS, HEAD_SIZE)

    pre_rows = prompt_cache.shape[2]
    suf_rows = request_cache.shape[2]
    first_group = (group_ids == 0)[:, None, None]
    pre_k = jnp.where(first_group, prompt_cache[0, 0][None], prompt_cache[0, 1][None])
    pre_v = jnp.where(first_group, prompt_cache[1, 0][None], prompt_cache[1, 1][None])
    keys = jnp.concatenate([pre_k, request_cache[0]], axis=1).reshape(
        request_count, pre_rows + suf_rows, KEY_VALUE_HEADS, HEAD_SIZE
    )
    values = jnp.concatenate([pre_v, request_cache[1]], axis=1).reshape(
        request_count, pre_rows + suf_rows, KEY_VALUE_HEADS, HEAD_SIZE
    )
    own_prefix = jnp.where(group_ids == 0, prefix_len[0], prefix_len[1])
    pre_pos = s * pre_rows + jnp.arange(pre_rows, dtype=jnp.int32)
    suf_pos = s * suf_rows + jnp.arange(suf_rows, dtype=jnp.int32)
    valid = jnp.concatenate(
        [pre_pos[None, :] < own_prefix[:, None], suf_pos[None, :] < suffix_len[:, None]], axis=1
    )[:, None, None, None, :]
    score_scale = 1.0 / math.sqrt(HEAD_SIZE)
    scores = jnp.einsum("jtkgd,jpkd->jtkgp", q, keys, preferred_element_type=jnp.float32) * score_scale
    scores = jnp.where(valid, scores, NEG)
    block_max = jnp.max(scores, axis=-1)
    probs = jnp.where(valid, jnp.exp(scores - block_max[..., None]), 0.0)
    block_sum = jnp.sum(probs, axis=-1)
    block_acc = jnp.einsum(
        "jtkgp,jpkd->jtkgd", probs.astype(jnp.bfloat16), values, preferred_element_type=jnp.float32
    )

    new_scores = jnp.einsum("jtkgd,jukd->jtkgu", q, k_new, preferred_element_type=jnp.float32) * score_scale
    causal = (jnp.arange(NEW_TOKENS)[:, None] >= jnp.arange(NEW_TOKENS)[None, :])[None, :, None, None, :]
    new_scores = jnp.where(causal, new_scores, NEG)
    new_max = jnp.max(new_scores, axis=-1)
    new_probs = jnp.where(causal, jnp.exp(new_scores - new_max[..., None]), 0.0)
    new_sum = jnp.sum(new_probs, axis=-1)
    new_acc = jnp.einsum(
        "jtkgu,jukd->jtkgd", new_probs.astype(jnp.bfloat16), v_new, preferred_element_type=jnp.float32
    )

    fs = qf // n_seq
    acc_flat = block_acc.reshape(attn_rows, qf)
    acc_parts = acc_flat.reshape(attn_rows, n_seq, fs).transpose(1, 0, 2)
    head_pick = np.array([[(i * fs) // HEAD_SIZE, (i * fs + fs - 1) // HEAD_SIZE] for i in range(n_seq)])
    max_flat = block_max.reshape(attn_rows, QUERY_HEADS)
    sum_flat = block_sum.reshape(attn_rows, QUERY_HEADS)
    max_parts = max_flat[:, head_pick].transpose(1, 0, 2)
    sum_parts = sum_flat[:, head_pick].transpose(1, 0, 2)
    merged = exchange(jnp.concatenate([acc_parts, max_parts, sum_parts], axis=-1), "seq")
    got_acc = merged[..., :fs]
    feat_ids = s * fs + jnp.arange(fs, dtype=jnp.int32)
    second = (feat_ids // HEAD_SIZE - (s * fs) // HEAD_SIZE) == 1
    got_max = jnp.where(second, merged[..., fs + 1 : fs + 2], merged[..., fs : fs + 1])
    got_sum = jnp.where(second, merged[..., fs + 3 : fs + 4], merged[..., fs + 2 : fs + 3])
    own_heads = feat_ids // HEAD_SIZE
    n_max = jnp.take(new_max.reshape(attn_rows, QUERY_HEADS), own_heads, axis=1)
    n_sum = jnp.take(new_sum.reshape(attn_rows, QUERY_HEADS), own_heads, axis=1)
    n_acc = lax.dynamic_slice_in_dim(new_acc.reshape(attn_rows, qf), s * fs, fs, 1)
    overall = jnp.maximum(jnp.max(got_max, axis=0), n_max)
    cache_weight = jnp.exp(got_max - overall)
    own_weight = jnp.exp(n_max - overall)
    denominator = jnp.sum(cache_weight * got_sum, axis=0) + own_weight * n_sum
    numerator = jnp.sum(cache_weight * got_acc, axis=0) + own_weight * n_acc
    attended = (numerator / denominator).astype(jnp.bfloat16)

    att_all = lax.all_gather(attended, "mp", axis=0, tiled=True)
    out_part = jnp.dot(att_all, w_out, preferred_element_type=jnp.float32)
    out_got = exchange(out_part.reshape(n_seq, home_rows, out_part.shape[-1]), "seq")
    x2 = (x_home + jnp.sum(out_got, axis=0)).astype(jnp.bfloat16)

    route_blocks = routes.reshape(n_seq, home_rows, TOPK)
    experts_all = jnp.arange(E, dtype=jnp.int32)
    hit = jnp.any(route_blocks[:, :, :, None] == experts_all, axis=2)
    hit_count = hit.astype(jnp.int32)
    ahead = jnp.cumsum(hit_count, axis=1) - hit_count
    chosen = hit[..., None] & (ahead[..., None] == jnp.arange(MOST, dtype=jnp.int32))
    chosen = jnp.transpose(chosen, (0, 2, 3, 1)).astype(jnp.bfloat16)
    member = hit.astype(jnp.bfloat16)

    home_table = chosen[s]
    dispatch = jnp.einsum("esr,rf->esf", home_table, x2, preferred_element_type=jnp.float32).astype(
        jnp.bfloat16
    )
    slot_rows = exchange(dispatch, "seq")
    slot_full = lax.all_gather(slot_rows, "mp", axis=2, tiled=True).reshape(n_seq * MOST, D)

    expert = s
    expert_table = chosen[:, expert]
    slot_member = jnp.einsum(
        "bsr,bre->bse", expert_table, member, preferred_element_type=jnp.float32
    ).reshape(n_seq * MOST, E)
    floats2 = slot_full.astype(jnp.float32)
    mean_sq = jnp.mean(floats2 * floats2, axis=-1, keepdims=True)
    normed2 = (floats2 * lax.rsqrt(mean_sq + EPS) * moe_gain).astype(jnp.bfloat16)
    logits = jnp.dot(normed2, w_router, preferred_element_type=jnp.float32)
    which = (experts_all == expert).astype(jnp.float32)
    own_flag = jnp.sum(slot_member * which, axis=1)
    own_logit = jnp.sum(logits * which, axis=1)
    denom = jnp.sum(jnp.where(slot_member > 0, jnp.exp(logits), 0.0), axis=1)
    share = own_flag * jnp.exp(own_logit) / (denom + 1.0 - own_flag)

    gate_up = w_gate_up[0]
    half = gate_up.shape[1]
    both = lax.dot_general(
        normed2,
        gate_up.reshape(2 * half, D),
        (((1,), (1,)), ((), ())),
        preferred_element_type=jnp.float32,
    )
    hidden = (jnp.maximum(both[:, :half], 0.0) * both[:, half:]).astype(jnp.bfloat16)
    down_part = jnp.dot(hidden, w_down[0], preferred_element_type=jnp.float32).astype(jnp.bfloat16)
    down_got = exchange(
        down_part.reshape(n_seq * MOST, n_mp, feat_mp).transpose(1, 0, 2), "mp"
    )
    expert_out = jnp.sum(down_got.astype(jnp.float32), axis=0).astype(jnp.bfloat16)
    weighted = (share[:, None] * expert_out.astype(jnp.float32)).astype(jnp.bfloat16)
    back = exchange(weighted.reshape(n_seq, MOST, feat_mp), "seq")
    terms = jnp.einsum("esr,esf->rf", home_table, back, preferred_element_type=jnp.float32)
    final = (x2.astype(jnp.float32) + terms).astype(jnp.bfloat16)
    return final.reshape(home_rows // NEW_TOKENS, NEW_TOKENS, feat_mp)


def solution(mesh):
    in_specs = (
        P(),
        P("seq", "mp"),
        P("mp"),
        P("mp", "seq"),
        P("seq", "mp"),
        P(None, "mp", "seq", None),
        P(None, "mp", "seq", None),
        P("mp"),
        P("mp"),
        P("mp"),
        P(),
        P(),
        P("seq", None, "mp", None),
        P("seq", "mp", None),
        P(),
    )
    out_specs = P("seq", None, "mp")
    return jax.shard_map(
        on_device, mesh=mesh, in_specs=in_specs, out_specs=out_specs, check_vma=False
    )
```

time: 1150 us -> 343 us (0.30)
  waiting for transfers between devices: 692 us -> 58.9 us
  blocking collectives: 389 us -> 189 us
  starting transfers between devices: 0.43 us -> 37.1 us
  between operations: 14.7 us -> 0.9 us
    unnamed x10 -> x0, waiting for transfers between devices: 341 us -> none
    reduce_scatter x2 -> x0, waiting for transfers between devices: 155 us -> none  [the longest x1 102 us: on_device(): lax.psum_scatter(jnp.dot(row_block, w_out, preferred_element_type=jnp.flo...]
    psum x1 -> x0, waiting for transfers between devices: 132 us -> none  [on_device(): lax.psum((block_sum * rescale, block_acc * rescale[..., None]), 'seq')]
    pmax x1 -> x0, blocking collectives: 121 us -> none  [on_device(): merged_max = lax.pmax(block_max, 'seq')]
    psum x2 -> x1, blocking collectives: 148 us -> 27.4 us  [on_device(): square_sum = lax.psum(jnp.sum(x_home * x_home, axis=-1), 'mp')]
    all_gather x1 -> x0, waiting for transfers between devices: 64.4 us -> none  [on_device(): full_rows = lax.all_gather(rows_seq, 'mp', axis=2, tiled=True)]
    all_to_all x0 -> x5, waiting for transfers between devices: none -> 58.9 us  [exchange(): return lax.all_to_all(values, axis, 0, 0, tiled=True)]
    all_to_all x0 -> x5, starting transfers between devices: none -> 37.1 us  [exchange(): return lax.all_to_all(values, axis, 0, 0, tiled=True)]
  transfers between devices with their start and end apart: 7 -> 5, of which waited for: 7 -> 5; matrix products, arithmetic and copies ran while one was open for 1% -> 5% of each run, Pallas kernels for 0% -> 0%
where the time goes in v1:
time: 343 us; the launch traced here: 342 us
  blocking collectives  189 us (55%)
  waiting for transfers between devices  58.9 us (17%)
  starting transfers between devices  37.1 us (11%)
  local copies, waits for them, and re-layouts  31.9 us (9%)
  other arithmetic  15.9 us (5%)
  matrix products  8.57 us (2%)
    all_to_all x5, waiting for transfers between devices, exchange(): return lax.all_to_all(values, axis, 0, 0, tiled=True)  58.9 us
    all_gather x1, blocking collectives, on_device(): lax.all_gather(slot_rows, 'mp', axis=2, tiled=True).reshape(n_seq * MOST, D)  45.7 us
    all_to_all x5, starting transfers between devices, exchange(): return lax.all_to_all(values, axis, 0, 0, tiled=True)  37.1 us
    all_gather x1, blocking collectives, on_device(): normed_all = lax.all_gather(normed, 'seq', axis=0, tiled=True)  32 us
    all_to_all x2, blocking collectives, exchange(): return lax.all_to_all(values, axis, 0, 0, tiled=True)  29.8 us
    all_gather x1, blocking collectives, on_device(): qkv_rows = lax.all_gather(qkv_cols, 'seq', axis=1, tiled=True)  29.1 us
    psum x1, blocking collectives, on_device(): square_sum = lax.psum(jnp.sum(x_home * x_home, axis=-1), 'mp')  27.4 us
    all_gather x1, blocking collectives, on_device(): att_all = lax.all_gather(attended, 'mp', axis=0, tiled=True)  24.4 us
  transfers between devices with their start and end apart: 5, of which 5 were waited for; matrix products, arithmetic and copies ran while one was open for 5% of the time, Pallas kernels for 0%

profile of v1, /device:TPU:1, one launch (start us, length us, event | category | flops | bytes accessed | tf_op | source)
XLA Modules:
  0.0 341.7 jit_solution(17688282065486856965)
XLA Ops:
  2.2 2.2 copy.150
  4.4 3.2 gather_fusion
  8.6 10.5 %all-to-all-start = ((bf16[32,32,96]{2,1,0:T(8,128)(2,1)}), bf16[32,32,96]{2,1,0:T(8,128)(2,1)S(1)}, u32[]{:S(2)}, u32[]{:S(2)}) async-start(bf16[32,32,96]{2,1,0:T(8,128)(2,1)} %select_select_fusion), calls=%async_computation | async-start | bytes 524288 | tf_op jit(solution)/shard_map/all_to_all | solution.py:24
  28.4 27.4 %psum.7 = f32[32]{0:T(128)S(1)} all-reduce(f32[32]{0:T(128)S(1)} %multiply_reduce_fusion.2), channel_id=1, replica_groups=mesh['seq'=32,'mp'=16] {'mp'}, use_global_device_ids=true, to_apply=%region_2.3 | all-reduce | flops 32 | bytes 256 | tf_op jit(solution)/shard_map/psum | solution.py:59
  55.8 32.0 %all_gather.12 = bf16[1024,96]{1,0:T(8,128)(2,1)S(1)} all-gather(bf16[32,96]{1,0:T(8,128)(2,1)S(1)} %multiply_convert_fusion), channel_id=1, replica_groups=mesh['seq'=32,'mp'=16] {'seq'}, dimensions={0}, use_global_device_ids=true | all-gather | bytes 202752 | tf_op jit(solution)/shard_map/all_gather | solution.py:61
  89.5 6.4 %all-to-all-start.1 = ((f32[16,1,4096]{2,1,0:T(1,128)}), f32[16,1,4096]{2,1,0:T(1,128)S(1)}, u32[]{:S(2)}, u32[]{:S(2)}) async-start(f32[16,1,4096]{2,1,0:T(1,128)} %reshape.313), calls=%async_computation.1 | async-start | bytes 524288 | tf_op jit(solution)/shard_map/all_to_all | solution.py:24
  96.8 13.2 %all-to-all-done.1 = f32[16,1,4096]{2,1,0:T(1,128)S(1)} async-done(((f32[16,1,4096]{2,1,0:T(1,128)}), f32[16,1,4096]{2,1,0:T(1,128)S(1)}, u32[]{:S(2)}, u32[]{:S(2)}) %all-to-all-start.1) | async-done | bytes 262176 | tf_op jit(solution)/shard_map/all_to_all | solution.py:24
  111.9 29.1 %all_gather.13 = bf16[64,2048]{0,1:T(8,128)(2,1)S(1)} all-gather(bf16[64,64]{0,1:T(8,128)(2,1)S(1)} %bitcast_reduce_fusion), channel_id=1, replica_groups=mesh['seq'=32,'mp'=16] {'seq'}, dimensions={1}, use_global_device_ids=true | all-gather | bytes 270336 | tf_op jit(solution)/shard_map/all_gather | solution.py:67
  148.4 1.6 pad_maximum_fusion
  150.0 1.8 copy.168
  153.2 4.4 %all-to-all-start.2 = ((f32[32,1,3328]{2,1,0:T(1,128)}), f32[32,1,3328]{2,1,0:T(1,128)S(1)}, u32[]{:S(2)}, u32[]{:S(2)}) async-start(f32[32,1,3328]{2,1,0:T(1,128)} %reshape.315), calls=%async_computation.2 | async-start | bytes 851968 | tf_op jit(solution)/shard_map/all_to_all | solution.py:24
  162.2 5.9 %all-to-all-done.2 = f32[32,1,3328]{2,1,0:T(1,128)S(1)} async-done(((f32[32,1,3328]{2,1,0:T(1,128)}), f32[32,1,3328]{2,1,0:T(1,128)S(1)}, u32[]{:S(2)}, u32[]{:S(2)}) %all-to-all-start.2) | async-done | bytes 426016 | tf_op jit(solution)/shard_map/all_to_all | solution.py:24
  168.2 1.5 reduce.4
  170.8 24.4 %all-gather = bf16[16,64,48]{1,2,0:T(8,128)(2,1)S(1)} all-gather(bf16[1,64,48]{1,2,0:T(8,128)(2,1)S(1)} %fusion.63), channel_id=1, replica_groups=mesh['seq'=32,'mp'=16] {'mp'}, dimensions={0}, use_global_device_ids=true | all-gather | bytes 104448 | tf_op jit(solution)/shard_map/all_gather | solution.py:139
  196.6 10.6 %all-to-all-start.3 = ((f32[32,32,96]{2,1,0:T(8,128)}), f32[32,32,96]{2,1,0:T(8,128)S(1)}, u32[]{:S(2)}, u32[]{:S(2)}) async-start(f32[32,32,96]{2,1,0:T(8,128)} %bitcast.26), calls=%async_computation.3 | async-start | bytes 1048576 | tf_op jit(solution)/shard_map/all_to_all | solution.py:24
  209.3 9.6 %all-to-all-done.3 = f32[32,32,96]{2,1,0:T(8,128)S(1)} async-done(((f32[32,32,96]{2,1,0:T(8,128)}), f32[32,32,96]{2,1,0:T(8,128)S(1)}, u32[]{:S(2)}, u32[]{:S(2)}) %all-to-all-start.3) | async-done | bytes 393248 | tf_op jit(solution)/shard_map/all_to_all | solution.py:24
  219.2 10.8 %all_to_all.35 = bf16[32,8,96]{2,1,0:T(8,128)(2,1)S(1)} all-to-all(bf16[32,8,96]{2,1,0:T(8,128)(2,1)S(1)} %copy.198), channel_id=1, replica_groups=mesh['seq'=32,'mp'=16] {'seq'}, dimensions={0} | all-to-all | bytes 98304 | tf_op jit(solution)/shard_map/all_to_all | solution.py:24
  230.8 45.7 %all_gather.15 = bf16[32,8,1536]{0,1,2:T(8,128)(2,1)S(1)} all-gather(bf16[32,8,96]{0,1,2:T(8,128)(2,1)} %copy.199), channel_id=1, replica_groups=mesh['seq'=32,'mp'=16] {'mp'}, dimensions={2}, use_global_device_ids=true | all-gather | bytes 835584 | tf_op jit(solution)/shard_map/all_gather | solution.py:158
  276.5 3.6 %copy.200 = bf16[32,8,1536]{2,1,0:T(8,128)(2,1)} copy(bf16[32,8,1536]{0,1,2:T(8,128)(2,1)S(1)} %all_gather.15) | data formatting | bytes 1572864 | tf_op jit(solution)/shard_map/all_gather | solution.py:158
  280.1 1.4 fusion.5
  281.7 1.6 fusion.24
  284.9 5.1 %all-to-all-start.5 = ((bf16[16,256,96]{1,2,0:T(8,128)(2,1)}), bf16[16,256,96]{1,2,0:T(8,128)(2,1)S(1)}, u32[]{:S(2)}, u32[]{:S(2)}) async-start(bf16[16,256,96]{1,2,0:T(8,128)(2,1)} %bitcast.39), calls=%async_computation.5 | async-start | bytes 1572864 | tf_op jit(solution)/shard_map/all_to_all | solution.py:24
  292.0 29.6 %all-to-all-done.5 = bf16[16,256,96]{1,2,0:T(8,128)(2,1)S(1)} async-done(((bf16[16,256,96]{1,2,0:T(8,128)(2,1)}), bf16[16,256,96]{1,2,0:T(8,128)(2,1)S(1)}, u32[]{:S(2)}, u32[]{:S(2)}) %all-to-all-start.5) | async-done | bytes 786464 | tf_op jit(solution)/shard_map/all_to_all | solution.py:24
  321.8 19.1 %all_to_all.36 = bf16[32,8,96]{2,1,0:T(8,128)(2,1)S(1)} all-to-all(bf16[32,8,96]{2,1,0:T(8,128)(2,1)S(1)} %fusion.46), channel_id=1, replica_groups=mesh['seq'=32,'mp'=16] {'seq'}, dimensions={0} | all-to-all | bytes 98304 | tf_op jit(solution)/shard_map/all_to_all | solution.py:24
  (182 shorter events, 39.9 us)
Async XLA Ops:
  0.0 281.7 %copy-start = (bf16[1,2,48,1536]{3,2,1,0:T(8,128)(2,1)S(1)}, bf16[1,2,48,1536]{3,2,1,0:T(8,128)(2,1)}, u32[]{:S(2)}) copy-start(bf16[1,2,48,1536]{3,2,1,0:T(8,128)(2,1)} %param.32) | copy-start | bytes 884740
  4.4 16.0 %copy-start.13 = (s32[256,4,4]{0,2,1:T(4,128)S(1)}, s32[256,4,4]{0,2,1:T(4,128)}, u32[]{:S(2)}) copy-start(s32[256,4,4]{0,2,1:T(4,128)} %param.34) | copy-start | bytes 49156
  8.6 14.8 %copy-start.19 = (s32[2]{0:T(128)S(1)}, s32[2]{0:T(128)}, u32[]{:S(2)}) copy-start(s32[2]{0:T(128)} %param.28) | copy-start | bytes 28
  8.6 15.4 %copy-start.11 = (bf16[2,2,64,256]{3,2,1,0:T(8,128)(2,1)S(1)}, bf16[2,2,64,256]{3,2,1,0:T(8,128)(2,1)}, u32[]{:S(2)}) copy-start(bf16[2,2,64,256]{3,2,1,0:T(8,128)(2,1)} %param.25) | copy-start | bytes 393220
  8.6 19.6 %all-to-all-start = ((bf16[32,32,96]{2,1,0:T(8,128)(2,1)}), bf16[32,32,96]{2,1,0:T(8,128)(2,1)S(1)}, u32[]{:S(2)}, u32[]{:S(2)}) async-start(bf16[32,32,96]{2,1,0:T(8,128)(2,1)} %select_select_fusion), calls=%async_computation | async-start | bytes 524288 | tf_op jit(solution)/shard_map/all_to_all | solution.py:24
  25.8 30.0 %copy-start.20 = (f32[96]{0:T(128)S(1)}, f32[96]{0:T(128)}, u32[]{:S(2)}) copy-start(f32[96]{0:T(128)} %param.22) | copy-start | bytes 1156
  25.9 62.0 %copy-start.14 = (bf16[96,64]{0,1:T(8,128)(2,1)S(1)}, bf16[96,64]{0,1:T(8,128)(2,1)}, u32[]{:S(2)}) copy-start(bf16[96,64]{0,1:T(8,128)(2,1)} %param.23) | copy-start | bytes 36868
  88.1 7.8 %copy-start.23 = (s32[16]{0:T(128)S(1)}, s32[16]{0:T(128)}, u32[]{:S(2)}) copy-start(s32[16]{0:T(128)} %param.29) | copy-start | bytes 196
  88.1 8.5 %copy-start.21 = (s32[64]{0:T(128)S(1)}, s32[64]{0:T(128)}, u32[]{:S(2)}) copy-start(s32[64]{0:T(128)} %constant.117) | copy-start | bytes 772
  89.5 20.6 %all-to-all-start.1 = ((f32[16,1,4096]{2,1,0:T(1,128)}), f32[16,1,4096]{2,1,0:T(1,128)S(1)}, u32[]{:S(2)}, u32[]{:S(2)}) async-start(f32[16,1,4096]{2,1,0:T(1,128)} %reshape.313), calls=%async_computation.1 | async-start | bytes 524288 | tf_op jit(solution)/shard_map/all_to_all | solution.py:24
  151.9 5.7 %copy-start.9 = (bf16[16,4,2,6,128]{4,3,2,1,0:T(8,128)(2,1)S(1)}, bf16[16,4,2,6,128]{4,3,2,1,0:T(8,128)(2,1)}, u32[]{:S(2)}) copy-start(bf16[16,4,2,6,128]{4,3,2,1,0:T(8,128)(2,1)} %copy-done.8) | copy-start | bytes 589828
  151.9 5.7 %copy-start.12 = (bf16[16,4,2,128]{3,2,1,0:T(2,128)(2,1)S(1)}, bf16[16,4,2,128]{3,2,1,0:T(2,128)(2,1)}, u32[]{:S(2)}) copy-start(bf16[16,4,2,128]{3,2,1,0:T(2,128)(2,1)} %reshape.243) | copy-start | bytes 98308
  151.9 5.7 %copy-start.17 = (pred[4,4]{1,0:T(4,128)(4,1)S(1)}, pred[4,4]{1,0:T(4,128)(4,1)}, u32[]{:S(2)}) copy-start(pred[4,4]{1,0:T(4,128)(4,1)} %iota_compare_fusion.2) | copy-start | bytes 52
  153.2 15.0 %all-to-all-start.2 = ((f32[32,1,3328]{2,1,0:T(1,128)}), f32[32,1,3328]{2,1,0:T(1,128)S(1)}, u32[]{:S(2)}, u32[]{:S(2)}) async-start(f32[32,1,3328]{2,1,0:T(1,128)} %reshape.315), calls=%async_computation.2 | async-start | bytes 851968 | tf_op jit(solution)/shard_map/all_to_all | solution.py:24
  162.0 8.1 %copy-start.18 = (pred[48]{0:T(512)(128)(4,1)S(1)}, pred[48]{0:T(512)(128)(4,1)}, u32[]{:S(2)}) copy-start(pred[48]{0:T(512)(128)(4,1)} %subtract_compare_fusion) | copy-start | bytes 148
  162.0 8.3 %copy-start.16 = (pred[48]{0:T(512)(128)(4,1)S(1)}, pred[48]{0:T(512)(128)(4,1)}, u32[]{:S(2)}) copy-start(pred[48]{0:T(512)(128)(4,1)} %compare_and_fusion.2) | copy-start | bytes 148
  169.7 25.8 %copy-start.15 = (bf16[48,96]{1,0:T(8,128)(2,1)S(1)}, bf16[48,96]{1,0:T(8,128)(2,1)}, u32[]{:S(2)}) copy-start(bf16[48,96]{1,0:T(8,128)(2,1)} %param.24) | copy-start | bytes 27652
  170.7 36.5 %copy-start.2 = (s32[32,32,32]{1,0,2:T(8,128)S(1)}, s32[32,32,32]{1,0,2:T(8,128)}, u32[]{:S(2)}) copy-start(s32[32,32,32]{1,0,2:T(8,128)} %copy.196) | copy-start | bytes 393220
  170.7 36.5 %copy-start.7 = (pred[32,32,32]{1,0,2:T(8,128)(4,1)S(1)}, pred[32,32,32]{1,0,2:T(8,128)(4,1)}, u32[]{:S(2)}) copy-start(pred[32,32,32]{1,0,2:T(8,128)(4,1)} %copy.194) | copy-start | bytes 98308
  196.6 22.2 %all-to-all-start.3 = ((f32[32,32,96]{2,1,0:T(8,128)}), f32[32,32,96]{2,1,0:T(8,128)S(1)}, u32[]{:S(2)}, u32[]{:S(2)}) async-start(f32[32,32,96]{2,1,0:T(8,128)} %bitcast.26), calls=%async_computation.3 | async-start | bytes 1048576 | tf_op jit(solution)/shard_map/all_to_all | solution.py:24
  283.7 6.3 %copy-start.4 = (pred[32,32,32]{2,1,0:T(8,128)(4,1)S(1)}, pred[32,32,32]{2,1,0:T(8,128)(4,1)}, u32[]{:S(2)}) copy-start(pred[32,32,32]{2,1,0:T(8,128)(4,1)} %copy-done.3) | copy-start | bytes 98308
  283.7 7.6 %copy-start.1 = (bf16[32,8,1536]{2,1,0:T(8,128)(2,1)S(1)}, bf16[32,8,1536]{2,1,0:T(8,128)(2,1)}, u32[]{:S(2)}) copy-start(bf16[32,8,1536]{2,1,0:T(8,128)(2,1)} %copy.200) | copy-start | bytes 2359300
  283.7 7.6 %copy-start.24 = (bf16[1536,32]{0,1:T(8,128)(2,1)S(1)}, bf16[1536,32]{0,1:T(8,128)(2,1)}, u32[]{:S(2)}) copy-start(bf16[1536,32]{0,1:T(8,128)(2,1)} %param.31) | copy-start | bytes 294916
  284.9 36.6 %all-to-all-start.5 = ((bf16[16,256,96]{1,2,0:T(8,128)(2,1)}), bf16[16,256,96]{1,2,0:T(8,128)(2,1)S(1)}, u32[]{:S(2)}, u32[]{:S(2)}) async-start(bf16[16,256,96]{1,2,0:T(8,128)(2,1)} %bitcast.39), calls=%async_computation.5 | async-start | bytes 1572864 | tf_op jit(solution)/shard_map/all_to_all | solution.py:24
  (7 other events, 18.9 us)

commit v2 on v1

--- a/solution.py
+++ b/solution.py
@@ -22,6 +22,10 @@
 
 def exchange(values, axis):
     return lax.all_to_all(values, axis, 0, 0, tiled=True)
+
+
+def gather_by_exchange(values, axis, n):
+    return lax.all_to_all(jnp.broadcast_to(values[None], (n,) + values.shape), axis, 0, 0, tiled=True)
 
 
 def on_device(
@@ -56,15 +60,15 @@
     got = exchange(looked.reshape(n_seq, home_rows, feat_mp), "seq")
     x_home = jnp.sum(got.astype(jnp.float32), axis=0)
 
-    square_sum = lax.psum(jnp.sum(x_home * x_home, axis=-1), "mp")
+    square_sum = jnp.sum(gather_by_exchange(jnp.sum(x_home * x_home, axis=-1), "mp", n_mp), axis=0)
     normed = (x_home * lax.rsqrt(square_sum[:, None] / D + EPS) * attn_gain).astype(jnp.bfloat16)
-    normed_all = lax.all_gather(normed, "seq", axis=0, tiled=True)
+    normed_all = gather_by_exchange(normed, "seq", n_seq).reshape(total_rows, feat_mp)
 
     qkv_part = jnp.dot(normed_all, w_qkv, preferred_element_type=jnp.float32)
     attn_rows = total_rows // n_mp
     qkv_got = exchange(qkv_part.reshape(n_mp, attn_rows, qkv_part.shape[-1]), "mp")
     qkv_cols = jnp.sum(qkv_got, axis=0).astype(jnp.bfloat16)
-    qkv_rows = lax.all_gather(qkv_cols, "seq", axis=1, tiled=True)
+    qkv_rows = gather_by_exchange(qkv_cols, "seq", n_seq).transpose(1, 0, 2).reshape(attn_rows, -1)
 
     request_count = group_ids.shape[0]
     groups_per = QUERY_HEADS // KEY_VALUE_HEADS
@@ -136,7 +140,7 @@
     numerator = jnp.sum(cache_weight * got_acc, axis=0) + own_weight * n_acc
     attended = (numerator / denominator).astype(jnp.bfloat16)
 
-    att_all = lax.all_gather(attended, "mp", axis=0, tiled=True)
+    att_all = gather_by_exchange(attended, "mp", n_mp).reshape(total_rows, fs)
     out_part = jnp.dot(att_all, w_out, preferred_element_type=jnp.float32)
     out_got = exchange(out_part.reshape(n_seq, home_rows, out_part.shape[-1]), "seq")
     x2 = (x_home + jnp.sum(out_got, axis=0)).astype(jnp.bfloat16)
@@ -155,7 +159,7 @@
         jnp.bfloat16
     )
     slot_rows = exchange(dispatch, "seq")
-    slot_full = lax.all_gather(slot_rows, "mp", axis=2, tiled=True).reshape(n_seq * MOST, D)
+    slot_full = gather_by_exchange(slot_rows, "mp", n_mp).transpose(1, 2, 0, 3).reshape(n_seq * MOST, D)
 
     expert = s
     expert_table = chosen[:, expert]

time: 343 us -> 309 us (0.901)
  blocking collectives: 189 us -> 26.5 us
  waiting for transfers between devices: 58.9 us -> 144 us
  starting transfers between devices: 37.1 us -> 71.8 us
  local copies, waits for them, and re-layouts: 31.9 us -> 38.9 us
    all_gather x4 -> x0, blocking collectives: 131 us -> none  [the longest x1 45.7 us: on_device(): lax.all_gather(slot_rows, 'mp', axis=2, tiled=True).reshape(n_seq * MOST, D)]
    all_to_all x0 -> x5, waiting for transfers between devices: none -> 80.1 us  [gather_by_exchange(): lax.all_to_all(jnp.broadcast_to(values[None], (n,) + values.shape), axis,...]
    all_to_all x0 -> x5, starting transfers between devices: none -> 36.1 us  [gather_by_exchange(): lax.all_to_all(jnp.broadcast_to(values[None], (n,) + values.shape), axis,...]
    psum x1 -> x0, blocking collectives: 27.4 us -> none  [on_device(): square_sum = lax.psum(jnp.sum(x_home * x_home, axis=-1), 'mp')]
    all_to_all x5, waiting for transfers between devices: 58.9 us -> 64.2 us  [exchange(): return lax.all_to_all(values, axis, 0, 0, tiled=True)]
    convert_element_type x0 -> x3, local copies, waits for them, and re-layouts: none -> 4.57 us  [the longest x2 3.37 us: on_device(): floats2 = slot_full.astype(jnp.float32)]
    all_gather x2 -> x0, local copies, waits for them, and re-layouts: 3.7 us -> none  [the longest x1 3.65 us: on_device(): lax.all_gather(slot_rows, 'mp', axis=2, tiled=True).reshape(n_seq * MOST, D)]
    unnamed x61 -> x66, local copies, waits for them, and re-layouts: 6.82 us -> 7.84 us
  transfers between devices with their start and end apart: 5 -> 10, of which waited for: 5 -> 10; matrix products, arithmetic and copies ran while one was open for 5% -> 7% of each run, Pallas kernels for 0% -> 0%
where the time goes in v2:
time: 309 us; the launch traced here: 308 us
  waiting for transfers between devices  144 us (47%)
  starting transfers between devices  71.8 us (23%)
  local copies, waits for them, and re-layouts  38.9 us (13%)
  blocking collectives  26.5 us (9%)
  other arithmetic  15.7 us (5%)
  matrix products  9.55 us (3%)
    all_to_all x5, waiting for transfers between devices, gather_by_exchange(): lax.all_to_all(jnp.broadcast_to(values[None], (n,) + values.shape), axis,...  80.1 us
    all_to_all x5, waiting for transfers between devices, exchange(): return lax.all_to_all(values, axis, 0, 0, tiled=True)  64.2 us
    all_to_all x5, starting transfers between devices, gather_by_exchange(): lax.all_to_all(jnp.broadcast_to(values[None], (n,) + values.shape), axis,...  36.1 us
    all_to_all x5, starting transfers between devices, exchange(): return lax.all_to_all(values, axis, 0, 0, tiled=True)  35.7 us
    all_to_all x2, blocking collectives, exchange(): return lax.all_to_all(values, axis, 0, 0, tiled=True)  26.5 us
    unnamed x66, local copies, waits for them, and re-layouts  7.84 us
  transfers between devices with their start and end apart: 10, of which 10 were waited for; matrix products, arithmetic and copies ran while one was open for 7% of the time, Pallas kernels for 0%

profile of v2, /device:TPU:1, one launch (start us, length us, event | category | flops | bytes accessed | tf_op | source)
XLA Modules:
  0.0 307.8 jit_solution(2361974406013104410)
XLA Ops:
  2.2 2.2 copy.195
  4.4 3.2 %gather_fusion = bf16[1024,96]{1,0:T(8,128)(2,1)S(1)} fusion(bf16[4748,96]{1,0:T(8,128)(2,1)S(1)} %copy.195, s32[1024]{0:T(1024)S(1)} %broadcast_clamp_fusion), kind=kCustom, calls=%fused_computation.2 | custom fusion | bytes 397312 | tf_op jit(solution)/shard_map/jit(_take)/gather | solution.py:58
  8.6 10.4 %all-to-all-start = ((bf16[32,32,96]{2,1,0:T(8,128)(2,1)}), bf16[32,32,96]{2,1,0:T(8,128)(2,1)S(1)}, u32[]{:S(2)}, u32[]{:S(2)}) async-start(bf16[32,32,96]{2,1,0:T(8,128)(2,1)} %select_select_fusion), calls=%async_computation | async-start | bytes 524288 | tf_op jit(solution)/shard_map/all_to_all | solution.py:24
  20.2 7.8 %all-to-all-done = bf16[32,32,96]{2,1,0:T(8,128)(2,1)S(1)} async-done(((bf16[32,32,96]{2,1,0:T(8,128)(2,1)}), bf16[32,32,96]{2,1,0:T(8,128)(2,1)S(1)}, u32[]{:S(2)}, u32[]{:S(2)}) %all-to-all-start) | async-done | bytes 196640 | tf_op jit(solution)/shard_map/all_to_all | solution.py:24
  28.9 13.0 %all-to-all-start.1 = ((f32[16,1,32]{2,1,0:T(1,128)}), f32[16,1,32]{2,1,0:T(1,128)S(1)}, u32[]{:S(2)}, u32[]{:S(2)}) async-start(f32[16,1,32]{2,1,0:T(1,128)} %broadcast_in_dim.242), calls=%async_computation.1 | async-start | bytes 16384 | tf_op jit(solution)/shard_map/all_to_all | solution.py:28
  46.1 7.1 %all-to-all-done.1 = f32[16,1,32]{2,1,0:T(1,128)S(1)} async-done(((f32[16,1,32]{2,1,0:T(1,128)}), f32[16,1,32]{2,1,0:T(1,128)S(1)}, u32[]{:S(2)}, u32[]{:S(2)}) %all-to-all-start.1) | async-done | bytes 2080 | tf_op jit(solution)/shard_map/all_to_all | solution.py:28
  54.0 5.1 %all-to-all-start.2 = ((bf16[32,32,96]{2,1,0:T(8,128)(2,1)}), bf16[32,32,96]{2,1,0:T(8,128)(2,1)S(1)}, u32[]{:S(2)}, u32[]{:S(2)}) async-start(bf16[32,32,96]{2,1,0:T(8,128)(2,1)} %broadcast_in_dim.243), calls=%async_computation.2 | async-start | bytes 524288 | tf_op jit(solution)/shard_map/all_to_all | solution.py:28
  59.8 8.4 %all-to-all-done.2 = bf16[32,32,96]{2,1,0:T(8,128)(2,1)S(1)} async-done(((bf16[32,32,96]{2,1,0:T(8,128)(2,1)}), bf16[32,32,96]{2,1,0:T(8,128)(2,1)S(1)}, u32[]{:S(2)}, u32[]{:S(2)}) %all-to-all-start.2) | async-done | bytes 196640 | tf_op jit(solution)/shard_map/all_to_all | solution.py:28
  69.5 3.7 %all-to-all-start.3 = ((f32[16,1,4096]{2,1,0:T(1,128)}), f32[16,1,4096]{2,1,0:T(1,128)S(1)}, u32[]{:S(2)}, u32[]{:S(2)}) async-start(f32[16,1,4096]{2,1,0:T(1,128)} %reshape.363), calls=%async_computation.3 | async-start | bytes 524288 | tf_op jit(solution)/shard_map/all_to_all | solution.py:24
  75.3 12.0 %all-to-all-done.3 = f32[16,1,4096]{2,1,0:T(1,128)S(1)} async-done(((f32[16,1,4096]{2,1,0:T(1,128)}), f32[16,1,4096]{2,1,0:T(1,128)S(1)}, u32[]{:S(2)}, u32[]{:S(2)}) %all-to-all-start.3) | async-done | bytes 262176 | tf_op jit(solution)/shard_map/all_to_all | solution.py:24
  90.7 8.5 %all-to-all-start.4 = ((bf16[32,2,2048]{2,1,0:T(2,128)(2,1)}), bf16[32,2,2048]{2,1,0:T(2,128)(2,1)S(1)}, u32[]{:S(2)}, u32[]{:S(2)}) async-start(bf16[32,2,2048]{2,1,0:T(2,128)(2,1)} %reshape.365), calls=%async_computation.4 | async-start | bytes 524288 | tf_op jit(solution)/shard_map/all_to_all | solution.py:28
  99.4 8.9 %all-to-all-done.4 = bf16[32,2,2048]{2,1,0:T(2,128)(2,1)S(1)} async-done(((bf16[32,2,2048]{2,1,0:T(2,128)(2,1)}), bf16[32,2,2048]{2,1,0:T(2,128)(2,1)S(1)}, u32[]{:S(2)}, u32[]{:S(2)}) %all-to-all-start.4) | async-done | bytes 262176 | tf_op jit(solution)/shard_map/all_to_all | solution.py:28
  122.7 3.7 %all-to-all-start.5 = ((f32[32,1,3328]{2,1,0:T(1,128)}), f32[32,1,3328]{2,1,0:T(1,128)S(1)}, u32[]{:S(2)}, u32[]{:S(2)}) async-start(f32[32,1,3328]{2,1,0:T(1,128)} %reshape.367), calls=%async_computation.5 | async-start | bytes 851968 | tf_op jit(solution)/shard_map/all_to_all | solution.py:24
  131.0 6.1 %all-to-all-done.5 = f32[32,1,3328]{2,1,0:T(1,128)S(1)} async-done(((f32[32,1,3328]{2,1,0:T(1,128)}), f32[32,1,3328]{2,1,0:T(1,128)S(1)}, u32[]{:S(2)}, u32[]{:S(2)}) %all-to-all-start.5) | async-done | bytes 426016 | tf_op jit(solution)/shard_map/all_to_all | solution.py:24
  140.8 5.7 %all-to-all-start.6 = ((bf16[16,2,1536]{2,1,0:T(2,128)(2,1)}), bf16[16,2,1536]{2,1,0:T(2,128)(2,1)S(1)}, u32[]{:S(2)}, u32[]{:S(2)}) async-start(bf16[16,2,1536]{2,1,0:T(2,128)(2,1)} %reshape.369), calls=%async_computation.6 | async-start | bytes 196608 | tf_op jit(solution)/shard_map/all_to_all | solution.py:28
  148.4 10.4 %all-to-all-done.6 = bf16[16,2,1536]{2,1,0:T(2,128)(2,1)S(1)} async-done(((bf16[16,2,1536]{2,1,0:T(2,128)(2,1)}), bf16[16,2,1536]{2,1,0:T(2,128)(2,1)S(1)}, u32[]{:S(2)}, u32[]{:S(2)}) %all-to-all-start.6) | async-done | bytes 98336 | tf_op jit(solution)/shard_map/all_to_all | solution.py:28
  160.2 5.4 %all-to-all-start.7 = ((f32[32,32,96]{2,1,0:T(8,128)}), f32[32,32,96]{2,1,0:T(8,128)S(1)}, u32[]{:S(2)}, u32[]{:S(2)}) async-start(f32[32,32,96]{2,1,0:T(8,128)} %fusion.57), calls=%async_computation.7 | async-start | bytes 1048576 | tf_op jit(solution)/shard_map/all_to_all | solution.py:24
  166.6 10.5 %all-to-all-done.7 = f32[32,32,96]{2,1,0:T(8,128)S(1)} async-done(((f32[32,32,96]{2,1,0:T(8,128)}), f32[32,32,96]{2,1,0:T(8,128)S(1)}, u32[]{:S(2)}, u32[]{:S(2)}) %all-to-all-start.7) | async-done | bytes 393248 | tf_op jit(solution)/shard_map/all_to_all | solution.py:24
  177.4 10.8 %all_to_all.61 = bf16[32,8,96]{2,1,0:T(8,128)(2,1)S(1)} all-to-all(bf16[32,8,96]{2,1,0:T(8,128)(2,1)S(1)} %copy.239), channel_id=1, replica_groups=mesh['seq'=32,'mp'=16] {'seq'}, dimensions={0} | all-to-all | bytes 98304 | tf_op jit(solution)/shard_map/all_to_all | solution.py:24
  189.5 3.8 %all-to-all-start.9 = ((bf16[16,32,8,96]{3,2,1,0:T(8,128)(2,1)}), bf16[16,32,8,96]{3,2,1,0:T(8,128)(2,1)S(1)}, u32[]{:S(2)}, u32[]{:S(2)}) async-start(bf16[16,32,8,96]{3,2,1,0:T(8,128)(2,1)} %broadcast_in_dim.261), calls=%async_computation.9 | async-start | bytes 2097152 | tf_op jit(solution)/shard_map/all_to_all | solution.py:28
  193.3 45.4 %all-to-all-done.9 = bf16[16,32,8,96]{3,2,1,0:T(8,128)(2,1)S(1)} async-done(((bf16[16,32,8,96]{3,2,1,0:T(8,128)(2,1)}), bf16[16,32,8,96]{3,2,1,0:T(8,128)(2,1)S(1)}, u32[]{:S(2)}, u32[]{:S(2)}) %all-to-all-start.9) | async-done | bytes 786464 | tf_op jit(solution)/shard_map/all_to_all | solution.py:28
  243.9 12.6 %all-to-all-start.10 = ((bf16[16,256,96]{1,2,0:T(8,128)(2,1)}), bf16[16,256,96]{1,2,0:T(8,128)(2,1)S(1)}, u32[]{:S(2)}, u32[]{:S(2)}) async-start(bf16[16,256,96]{1,2,0:T(8,128)(2,1)} %bitcast.43), calls=%async_computation.10 | async-start | bytes 1572864 | tf_op jit(solution)/shard_map/all_to_all | solution.py:24
  263.4 27.7 %all-to-all-done.10 = bf16[16,256,96]{1,2,0:T(8,128)(2,1)S(1)} async-done(((bf16[16,256,96]{1,2,0:T(8,128)(2,1)}), bf16[16,256,96]{1,2,0:T(8,128)(2,1)S(1)}, u32[]{:S(2)}, u32[]{:S(2)}) %all-to-all-start.10) | async-done | bytes 786464 | tf_op jit(solution)/shard_map/all_to_all | solution.py:24
  291.4 15.7 %all_to_all.62 = bf16[32,8,96]{2,1,0:T(8,128)(2,1)S(1)} all-to-all(bf16[32,8,96]{2,1,0:T(8,128)(2,1)S(1)} %fusion.38), channel_id=1, replica_groups=mesh['seq'=32,'mp'=16] {'seq'}, dimensions={0} | all-to-all | bytes 98304 | tf_op jit(solution)/shard_map/all_to_all | solution.py:24
  (198 shorter events, 58.8 us)
Async XLA Ops:
  0.0 242.0 %copy-start = (bf16[1,2,48,1536]{3,2,1,0:T(8,128)(2,1)S(1)}, bf16[1,2,48,1536]{3,2,1,0:T(8,128)(2,1)}, u32[]{:S(2)}) copy-start(bf16[1,2,48,1536]{3,2,1,0:T(8,128)(2,1)} %param.32) | copy-start | bytes 884740
  4.4 15.7 %copy-start.2 = (bf16[2,16,64,256]{3,2,1,0:T(8,128)(2,1)S(1)}, bf16[2,16,64,256]{3,2,1,0:T(8,128)(2,1)}, u32[]{:S(2)}) copy-start(bf16[2,16,64,256]{3,2,1,0:T(8,128)(2,1)} %param.26) | copy-start | bytes 3145732
  7.6 37.4 %copy-start.16 = (s32[256,4,4]{0,2,1:T(4,128)S(1)}, s32[256,4,4]{0,2,1:T(4,128)}, u32[]{:S(2)}) copy-start(s32[256,4,4]{0,2,1:T(4,128)} %param.34) | copy-start | bytes 49156
  8.6 19.4 %all-to-all-start = ((bf16[32,32,96]{2,1,0:T(8,128)(2,1)}), bf16[32,32,96]{2,1,0:T(8,128)(2,1)S(1)}, u32[]{:S(2)}, u32[]{:S(2)}) async-start(bf16[32,32,96]{2,1,0:T(8,128)(2,1)} %select_select_fusion), calls=%async_computation | async-start | bytes 524288 | tf_op jit(solution)/shard_map/all_to_all | solution.py:24
  28.9 24.3 %all-to-all-start.1 = ((f32[16,1,32]{2,1,0:T(1,128)}), f32[16,1,32]{2,1,0:T(1,128)S(1)}, u32[]{:S(2)}, u32[]{:S(2)}) async-start(f32[16,1,32]{2,1,0:T(1,128)} %broadcast_in_dim.242), calls=%async_computation.1 | async-start | bytes 16384 | tf_op jit(solution)/shard_map/all_to_all | solution.py:28
  45.7 22.6 %copy-start.17 = (bf16[96,64]{0,1:T(8,128)(2,1)S(1)}, bf16[96,64]{0,1:T(8,128)(2,1)}, u32[]{:S(2)}) copy-start(bf16[96,64]{0,1:T(8,128)(2,1)} %param.23) | copy-start | bytes 36868
  45.9 27.3 %copy-start.25 = (s32[16]{0:T(128)S(1)}, s32[16]{0:T(128)}, u32[]{:S(2)}) copy-start(s32[16]{0:T(128)} %param.27) | copy-start | bytes 196
  45.9 28.5 %copy-start.26 = (s32[16]{0:T(128)S(1)}, s32[16]{0:T(128)}, u32[]{:S(2)}) copy-start(s32[16]{0:T(128)} %param.29) | copy-start | bytes 196
  45.9 29.3 %copy-start.24 = (s32[64]{0:T(128)S(1)}, s32[64]{0:T(128)}, u32[]{:S(2)}) copy-start(s32[64]{0:T(128)} %constant.117) | copy-start | bytes 772
  54.0 14.2 %all-to-all-start.2 = ((bf16[32,32,96]{2,1,0:T(8,128)(2,1)}), bf16[32,32,96]{2,1,0:T(8,128)(2,1)S(1)}, u32[]{:S(2)}, u32[]{:S(2)}) async-start(bf16[32,32,96]{2,1,0:T(8,128)(2,1)} %broadcast_in_dim.243), calls=%async_computation.2 | async-start | bytes 524288 | tf_op jit(solution)/shard_map/all_to_all | solution.py:28
  69.5 29.8 %copy-start.7 = (bf16[64,2,128]{2,0,1:T(8,128)(2,1)S(1)}, bf16[64,2,128]{2,0,1:T(8,128)(2,1)}, u32[]{:S(2)}) copy-start(bf16[64,2,128]{2,0,1:T(8,128)(2,1)} %copy.196) | copy-start | bytes 98308
  69.5 29.8 %copy-start.8 = (bf16[64,2,128]{2,0,1:T(8,128)(2,1)S(1)}, bf16[64,2,128]{2,0,1:T(8,128)(2,1)}, u32[]{:S(2)}) copy-start(bf16[64,2,128]{2,0,1:T(8,128)(2,1)} %copy.197) | copy-start | bytes 98308
  69.5 29.8 %copy-start.9 = (bf16[64,2,128]{2,0,1:T(8,128)(2,1)S(1)}, bf16[64,2,128]{2,0,1:T(8,128)(2,1)}, u32[]{:S(2)}) copy-start(bf16[64,2,128]{2,0,1:T(8,128)(2,1)} %copy.200) | copy-start | bytes 98308
  69.5 29.8 %copy-start.10 = (bf16[64,2,128]{2,0,1:T(8,128)(2,1)S(1)}, bf16[64,2,128]{2,0,1:T(8,128)(2,1)}, u32[]{:S(2)}) copy-start(bf16[64,2,128]{2,0,1:T(8,128)(2,1)} %copy.199) | copy-start | bytes 98308
  69.5 17.8 %all-to-all-start.3 = ((f32[16,1,4096]{2,1,0:T(1,128)}), f32[16,1,4096]{2,1,0:T(1,128)S(1)}, u32[]{:S(2)}, u32[]{:S(2)}) async-start(f32[16,1,4096]{2,1,0:T(1,128)} %reshape.363), calls=%async_computation.3 | async-start | bytes 524288 | tf_op jit(solution)/shard_map/all_to_all | solution.py:24
  90.7 17.6 %all-to-all-start.4 = ((bf16[32,2,2048]{2,1,0:T(2,128)(2,1)}), bf16[32,2,2048]{2,1,0:T(2,128)(2,1)S(1)}, u32[]{:S(2)}, u32[]{:S(2)}) async-start(bf16[32,2,2048]{2,1,0:T(2,128)(2,1)} %reshape.365), calls=%async_computation.4 | async-start | bytes 524288 | tf_op jit(solution)/shard_map/all_to_all | solution.py:28
  122.7 14.4 %all-to-all-start.5 = ((f32[32,1,3328]{2,1,0:T(1,128)}), f32[32,1,3328]{2,1,0:T(1,128)S(1)}, u32[]{:S(2)}, u32[]{:S(2)}) async-start(f32[32,1,3328]{2,1,0:T(1,128)} %reshape.367), calls=%async_computation.5 | async-start | bytes 851968 | tf_op jit(solution)/shard_map/all_to_all | solution.py:24
  139.8 19.3 %copy-start.18 = (bf16[48,96]{1,0:T(8,128)(2,1)S(1)}, bf16[48,96]{1,0:T(8,128)(2,1)}, u32[]{:S(2)}) copy-start(bf16[48,96]{1,0:T(8,128)(2,1)} %param.24) | copy-start | bytes 27652
  140.8 18.0 %all-to-all-start.6 = ((bf16[16,2,1536]{2,1,0:T(2,128)(2,1)}), bf16[16,2,1536]{2,1,0:T(2,128)(2,1)S(1)}, u32[]{:S(2)}, u32[]{:S(2)}) async-start(bf16[16,2,1536]{2,1,0:T(2,128)(2,1)} %reshape.369), calls=%async_computation.6 | async-start | bytes 196608 | tf_op jit(solution)/shard_map/all_to_all | solution.py:28
  160.2 17.0 %all-to-all-start.7 = ((f32[32,32,96]{2,1,0:T(8,128)}), f32[32,32,96]{2,1,0:T(8,128)S(1)}, u32[]{:S(2)}, u32[]{:S(2)}) async-start(f32[32,32,96]{2,1,0:T(8,128)} %fusion.57), calls=%async_computation.7 | async-start | bytes 1048576 | tf_op jit(solution)/shard_map/all_to_all | solution.py:24
  166.4 72.7 %copy-start.1 = (pred[32,32,32,8]{1,3,0,2:T(8,128)(4,1)}, pred[32,32,32,8]{1,3,0,2:T(8,128)(4,1)S(1)}, u32[]{:S(2)}) copy-start(pred[32,32,32,8]{1,3,0,2:T(8,128)(4,1)S(1)} %fusion) | copy-start | bytes 786436
  166.6 26.7 %copy-start.14 = (f32[1536]{0:T(1024)S(1)}, f32[1536]{0:T(1024)}, u32[]{:S(2)}) copy-start(f32[1536]{0:T(1024)} %param.30) | copy-start | bytes 18436
  189.5 49.3 %all-to-all-start.9 = ((bf16[16,32,8,96]{3,2,1,0:T(8,128)(2,1)}), bf16[16,32,8,96]{3,2,1,0:T(8,128)(2,1)S(1)}, u32[]{:S(2)}, u32[]{:S(2)}) async-start(bf16[16,32,8,96]{3,2,1,0:T(8,128)(2,1)} %broadcast_in_dim.261), calls=%async_computation.9 | async-start | bytes 2097152 | tf_op jit(solution)/shard_map/all_to_all | solution.py:28
  243.9 47.1 %all-to-all-start.10 = ((bf16[16,256,96]{1,2,0:T(8,128)(2,1)}), bf16[16,256,96]{1,2,0:T(8,128)(2,1)S(1)}, u32[]{:S(2)}, u32[]{:S(2)}) async-start(bf16[16,256,96]{1,2,0:T(8,128)(2,1)} %bitcast.43), calls=%async_computation.10 | async-start | bytes 1572864 | tf_op jit(solution)/shard_map/all_to_all | solution.py:24
  (13 other events, 85.9 us)

commit v3 on v2

--- a/solution.py
+++ b/solution.py
@@ -155,21 +155,21 @@
     member = hit.astype(jnp.bfloat16)
 
     home_table = chosen[s]
-    dispatch = jnp.einsum("esr,rf->esf", home_table, x2, preferred_element_type=jnp.float32).astype(
+    x2_full = gather_by_exchange(x2, "mp", n_mp).transpose(1, 0, 2).reshape(home_rows, D)
+    floats2 = x2_full.astype(jnp.float32)
+    mean_sq = jnp.mean(floats2 * floats2, axis=-1, keepdims=True)
+    normed2 = (floats2 * lax.rsqrt(mean_sq + EPS) * moe_gain).astype(jnp.bfloat16)
+    dispatch = jnp.einsum("esr,rf->esf", home_table, normed2, preferred_element_type=jnp.float32).astype(
         jnp.bfloat16
     )
-    slot_rows = exchange(dispatch, "seq")
-    slot_full = gather_by_exchange(slot_rows, "mp", n_mp).transpose(1, 2, 0, 3).reshape(n_seq * MOST, D)
+    slot_normed = exchange(dispatch, "seq").reshape(n_seq * MOST, D)
 
     expert = s
     expert_table = chosen[:, expert]
     slot_member = jnp.einsum(
         "bsr,bre->bse", expert_table, member, preferred_element_type=jnp.float32
     ).reshape(n_seq * MOST, E)
-    floats2 = slot_full.astype(jnp.float32)
-    mean_sq = jnp.mean(floats2 * floats2, axis=-1, keepdims=True)
-    normed2 = (floats2 * lax.rsqrt(mean_sq + EPS) * moe_gain).astype(jnp.bfloat16)
-    logits = jnp.dot(normed2, w_router, preferred_element_type=jnp.float32)
+    logits = jnp.dot(slot_normed, w_router, preferred_element_type=jnp.float32)
     which = (experts_all == expert).astype(jnp.float32)
     own_flag = jnp.sum(slot_member * which, axis=1)
     own_logit = jnp.sum(logits * which, axis=1)
@@ -179,17 +179,17 @@
     gate_up = w_gate_up[0]
     half = gate_up.shape[1]
     both = lax.dot_general(
-        normed2,
+        slot_normed,
         gate_up.reshape(2 * half, D),
         (((1,), (1,)), ((), ())),
         preferred_element_type=jnp.float32,
     )
     hidden = (jnp.maximum(both[:, :half], 0.0) * both[:, half:]).astype(jnp.bfloat16)
-    down_part = jnp.dot(hidden, w_down[0], preferred_element_type=jnp.float32).astype(jnp.bfloat16)
-    down_got = exchange(
-        down_part.reshape(n_seq * MOST, n_mp, feat_mp).transpose(1, 0, 2), "mp"
-    )
-    expert_out = jnp.sum(down_got.astype(jnp.float32), axis=0).astype(jnp.bfloat16)
+    hidden_all = gather_by_exchange(hidden, "mp", n_mp)
+    hidden_all = hidden_all.transpose(1, 0, 2).reshape(n_seq * MOST, n_mp * half)
+    down_cols = exchange(w_down[0].reshape(half, n_mp, feat_mp).transpose(1, 0, 2), "mp")
+    down_cols = down_cols.reshape(n_mp * half, feat_mp)
+    expert_out = jnp.dot(hidden_all, down_cols, preferred_element_type=jnp.float32).astype(jnp.bfloat16)
     weighted = (share[:, None] * expert_out.astype(jnp.float32)).astype(jnp.bfloat16)
     back = exchange(weighted.reshape(n_seq, MOST, feat_mp), "seq")
     terms = jnp.einsum("esr,esf->rf", home_table, back, preferred_element_type=jnp.float32)

time: 309 us -> 280 us (0.906)
  waiting for transfers between devices: 144 us -> 131 us
  blocking collectives: 26.5 us -> 17.6 us
  local copies, waits for them, and re-layouts: 38.9 us -> 31.4 us
  starting transfers between devices: 71.8 us -> 77.7 us
  other arithmetic: 15.7 us -> 12.6 us
    all_to_all x5 -> x6, waiting for transfers between devices: 80.1 us -> 66.9 us  [gather_by_exchange(): lax.all_to_all(jnp.broadcast_to(values[None], (n,) + values.shape), axis,...]
    all_to_all x2 -> x1, blocking collectives: 26.5 us -> 17.6 us  [exchange(): return lax.all_to_all(values, axis, 0, 0, tiled=True)]
    all_to_all x5 -> x6, starting transfers between devices: 36.1 us -> 44.2 us  [gather_by_exchange(): lax.all_to_all(jnp.broadcast_to(values[None], (n,) + values.shape), axis,...]
    convert_element_type x5 -> x1, local copies, waits for them, and re-layouts: 4.66 us -> 0.11 us  [on_device(): (share[:, None] * expert_out.astype(jnp.float32)).astype(jnp.bfloat16)]
    all_to_all x5 -> x6, starting transfers between devices: 35.7 us -> 33.5 us  [exchange(): return lax.all_to_all(values, axis, 0, 0, tiled=True)]
    all_to_all x5 -> x6, waiting for transfers between devices: 64.2 us -> 63.9 us  [exchange(): return lax.all_to_all(values, axis, 0, 0, tiled=True)]
    unnamed x66 -> x52, local copies, waits for them, and re-layouts: 7.84 us -> 7.8 us
  transfers between devices with their start and end apart: 10 -> 12, of which waited for: 10 -> 12; matrix products, arithmetic and copies ran while one was open for 7% -> 5% of each run, Pallas kernels for 0% -> 0%
where the time goes in v3:
time: 280 us; the launch traced here: 278 us
  waiting for transfers between devices  131 us (47%)
  starting transfers between devices  77.7 us (28%)
  local copies, waits for them, and re-layouts  31.4 us (11%)
  blocking collectives  17.6 us (6%)
  other arithmetic  12.6 us (4%)
  matrix products  7.31 us (3%)
    all_to_all x6, waiting for transfers between devices, gather_by_exchange(): lax.all_to_all(jnp.broadcast_to(values[None], (n,) + values.shape), axis,...  66.9 us
    all_to_all x6, waiting for transfers between devices, exchange(): return lax.all_to_all(values, axis, 0, 0, tiled=True)  63.9 us
    all_to_all x6, starting transfers between devices, gather_by_exchange(): lax.all_to_all(jnp.broadcast_to(values[None], (n,) + values.shape), axis,...  44.2 us
    all_to_all x6, starting transfers between devices, exchange(): return lax.all_to_all(values, axis, 0, 0, tiled=True)  33.5 us
    all_to_all x1, blocking collectives, exchange(): return lax.all_to_all(values, axis, 0, 0, tiled=True)  17.6 us
    unnamed x52, local copies, waits for them, and re-layouts  7.8 us
  transfers between devices with their start and end apart: 12, of which 12 were waited for; matrix products, arithmetic and copies ran while one was open for 5% of the time, Pallas kernels for 0%

profile of v3, /device:TPU:1, one launch (start us, length us, event | category | flops | bytes accessed | tf_op | source)
XLA Modules:
  0.0 278.4 jit_solution(1903189851006375838)
XLA Ops:
  8.6 10.5 %all-to-all-start = ((bf16[32,32,96]{2,1,0:T(8,128)(2,1)}), bf16[32,32,96]{2,1,0:T(8,128)(2,1)S(1)}, u32[]{:S(2)}, u32[]{:S(2)}) async-start(bf16[32,32,96]{2,1,0:T(8,128)(2,1)} %select_select_fusion), calls=%async_computation | async-start | bytes 524288 | tf_op jit(solution)/shard_map/all_to_all | solution.py:24
  19.3 8.8 %all-to-all-done = bf16[32,32,96]{2,1,0:T(8,128)(2,1)S(1)} async-done(((bf16[32,32,96]{2,1,0:T(8,128)(2,1)}), bf16[32,32,96]{2,1,0:T(8,128)(2,1)S(1)}, u32[]{:S(2)}, u32[]{:S(2)}) %all-to-all-start) | async-done | bytes 196640 | tf_op jit(solution)/shard_map/all_to_all | solution.py:24
  29.0 13.0 %all-to-all-start.1 = ((f32[16,1,32]{2,1,0:T(1,128)}), f32[16,1,32]{2,1,0:T(1,128)S(1)}, u32[]{:S(2)}, u32[]{:S(2)}) async-start(f32[16,1,32]{2,1,0:T(1,128)} %broadcast_in_dim.248), calls=%async_computation.1 | async-start | bytes 16384 | tf_op jit(solution)/shard_map/all_to_all | solution.py:28
  43.9 9.4 %all-to-all-done.1 = f32[16,1,32]{2,1,0:T(1,128)S(1)} async-done(((f32[16,1,32]{2,1,0:T(1,128)}), f32[16,1,32]{2,1,0:T(1,128)S(1)}, u32[]{:S(2)}, u32[]{:S(2)}) %all-to-all-start.1) | async-done | bytes 2080 | tf_op jit(solution)/shard_map/all_to_all | solution.py:28
  54.1 5.3 %all-to-all-start.2 = ((bf16[32,32,96]{2,1,0:T(8,128)(2,1)}), bf16[32,32,96]{2,1,0:T(8,128)(2,1)S(1)}, u32[]{:S(2)}, u32[]{:S(2)}) async-start(bf16[32,32,96]{2,1,0:T(8,128)(2,1)} %broadcast_in_dim.249), calls=%async_computation.2 | async-start | bytes 524288 | tf_op jit(solution)/shard_map/all_to_all | solution.py:28
  60.1 8.4 %all-to-all-done.2 = bf16[32,32,96]{2,1,0:T(8,128)(2,1)S(1)} async-done(((bf16[32,32,96]{2,1,0:T(8,128)(2,1)}), bf16[32,32,96]{2,1,0:T(8,128)(2,1)S(1)}, u32[]{:S(2)}, u32[]{:S(2)}) %all-to-all-start.2) | async-done | bytes 196640 | tf_op jit(solution)/shard_map/all_to_all | solution.py:28
  74.8 12.8 %all-to-all-done.3 = f32[16,1,4096]{2,1,0:T(1,128)S(1)} async-done(((f32[16,1,4096]{2,1,0:T(1,128)}), f32[16,1,4096]{2,1,0:T(1,128)S(1)}, u32[]{:S(2)}, u32[]{:S(2)}) %all-to-all-start.3) | async-done | bytes 262176 | tf_op jit(solution)/shard_map/all_to_all | solution.py:24
  90.9 8.2 %all-to-all-start.4 = ((bf16[32,2,2048]{2,1,0:T(2,128)(2,1)}), bf16[32,2,2048]{2,1,0:T(2,128)(2,1)S(1)}, u32[]{:S(2)}, u32[]{:S(2)}) async-start(bf16[32,2,2048]{2,1,0:T(2,128)(2,1)} %reshape.355), calls=%async_computation.4 | async-start | bytes 524288 | tf_op jit(solution)/shard_map/all_to_all | solution.py:28
  99.4 8.9 %all-to-all-done.4 = bf16[32,2,2048]{2,1,0:T(2,128)(2,1)S(1)} async-done(((bf16[32,2,2048]{2,1,0:T(2,128)(2,1)}), bf16[32,2,2048]{2,1,0:T(2,128)(2,1)S(1)}, u32[]{:S(2)}, u32[]{:S(2)}) %all-to-all-start.4) | async-done | bytes 262176 | tf_op jit(solution)/shard_map/all_to_all | solution.py:28
  121.8 3.9 %all-to-all-start.5 = ((f32[32,1,3328]{2,1,0:T(1,128)}), f32[32,1,3328]{2,1,0:T(1,128)S(1)}, u32[]{:S(2)}, u32[]{:S(2)}) async-start(f32[32,1,3328]{2,1,0:T(1,128)} %reshape.357), calls=%async_computation.5 | async-start | bytes 851968 | tf_op jit(solution)/shard_map/all_to_all | solution.py:24
  130.0 6.4 %all-to-all-done.5 = f32[32,1,3328]{2,1,0:T(1,128)S(1)} async-done(((f32[32,1,3328]{2,1,0:T(1,128)}), f32[32,1,3328]{2,1,0:T(1,128)S(1)}, u32[]{:S(2)}, u32[]{:S(2)}) %all-to-all-start.5) | async-done | bytes 426016 | tf_op jit(solution)/shard_map/all_to_all | solution.py:24
  140.0 5.6 %all-to-all-start.6 = ((bf16[16,2,1536]{2,1,0:T(2,128)(2,1)}), bf16[16,2,1536]{2,1,0:T(2,128)(2,1)S(1)}, u32[]{:S(2)}, u32[]{:S(2)}) async-start(bf16[16,2,1536]{2,1,0:T(2,128)(2,1)} %reshape.359), calls=%async_computation.6 | async-start | bytes 196608 | tf_op jit(solution)/shard_map/all_to_all | solution.py:28
  146.2 11.7 %all-to-all-done.6 = bf16[16,2,1536]{2,1,0:T(2,128)(2,1)S(1)} async-done(((bf16[16,2,1536]{2,1,0:T(2,128)(2,1)}), bf16[16,2,1536]{2,1,0:T(2,128)(2,1)S(1)}, u32[]{:S(2)}, u32[]{:S(2)}) %all-to-all-start.6) | async-done | bytes 98336 | tf_op jit(solution)/shard_map/all_to_all | solution.py:28
  159.3 5.3 %all-to-all-start.7 = ((f32[32,32,96]{2,1,0:T(8,128)}), f32[32,32,96]{2,1,0:T(8,128)S(1)}, u32[]{:S(2)}, u32[]{:S(2)}) async-start(f32[32,32,96]{2,1,0:T(8,128)} %fusion.60), calls=%async_computation.7 | async-start | bytes 1048576 | tf_op jit(solution)/shard_map/all_to_all | solution.py:24
  166.6 9.7 %all-to-all-done.7 = f32[32,32,96]{2,1,0:T(8,128)S(1)} async-done(((f32[32,32,96]{2,1,0:T(8,128)}), f32[32,32,96]{2,1,0:T(8,128)S(1)}, u32[]{:S(2)}, u32[]{:S(2)}) %all-to-all-start.7) | async-done | bytes 393248 | tf_op jit(solution)/shard_map/all_to_all | solution.py:24
  177.0 3.8 %all-to-all-start.8 = ((bf16[16,32,96]{2,1,0:T(8,128)(2,1)}), bf16[16,32,96]{2,1,0:T(8,128)(2,1)S(1)}, u32[]{:S(2)}, u32[]{:S(2)}) async-start(bf16[16,32,96]{2,1,0:T(8,128)(2,1)} %broadcast_in_dim.267), calls=%async_computation.8 | async-start | bytes 262144 | tf_op jit(solution)/shard_map/all_to_all | solution.py:28
  181.7 11.7 %all-to-all-done.8 = bf16[16,32,96]{2,1,0:T(8,128)(2,1)S(1)} async-done(((bf16[16,32,96]{2,1,0:T(8,128)(2,1)}), bf16[16,32,96]{2,1,0:T(8,128)(2,1)S(1)}, u32[]{:S(2)}, u32[]{:S(2)}) %all-to-all-start.8) | async-done | bytes 98336 | tf_op jit(solution)/shard_map/all_to_all | solution.py:28
  195.1 6.0 %all-to-all-start.9 = ((bf16[32,8,1536]{2,1,0:T(8,128)(2,1)}), bf16[32,8,1536]{2,1,0:T(8,128)(2,1)S(1)}, u32[]{:S(2)}, u32[]{:S(2)}) async-start(bf16[32,8,1536]{2,1,0:T(8,128)(2,1)} %convolution_convert_fusion), calls=%async_computation.9 | async-start | bytes 1572864 | tf_op jit(solution)/shard_map/all_to_all | solution.py:24
  202.0 13.3 %all-to-all-done.9 = bf16[32,8,1536]{2,1,0:T(8,128)(2,1)S(1)} async-done(((bf16[32,8,1536]{2,1,0:T(8,128)(2,1)}), bf16[32,8,1536]{2,1,0:T(8,128)(2,1)S(1)}, u32[]{:S(2)}, u32[]{:S(2)}) %all-to-all-start.9) | async-done | bytes 786464 | tf_op jit(solution)/shard_map/all_to_all | solution.py:24
  215.4 4.3 %all-to-all-start.11 = ((bf16[16,48,96]{2,1,0:T(8,128)(2,1)}), bf16[16,48,96]{2,1,0:T(8,128)(2,1)S(1)}, u32[]{:S(2)}, u32[]{:S(2)}) async-start(bf16[16,48,96]{2,1,0:T(8,128)(2,1)} %bitcast.161), calls=%async_computation.11 | async-start | bytes 393216 | tf_op jit(solution)/shard_map/all_to_all | solution.py:24
  220.0 12.8 %all-to-all-done.11 = bf16[16,48,96]{2,1,0:T(8,128)(2,1)S(1)} async-done(((bf16[16,48,96]{2,1,0:T(8,128)(2,1)}), bf16[16,48,96]{2,1,0:T(8,128)(2,1)S(1)}, u32[]{:S(2)}, u32[]{:S(2)}) %all-to-all-start.11) | async-done | bytes 147488 | tf_op jit(solution)/shard_map/all_to_all | solution.py:24
  233.6 8.3 %all-to-all-start.10 = ((bf16[16,256,48]{1,2,0:T(8,128)(2,1)}), bf16[16,256,48]{1,2,0:T(8,128)(2,1)S(1)}, u32[]{:S(2)}, u32[]{:S(2)}) async-start(bf16[16,256,48]{1,2,0:T(8,128)(2,1)} %broadcast_in_dim.268), calls=%async_computation.10 | async-start | bytes 786432 | tf_op jit(solution)/shard_map/all_to_all | solution.py:28
  242.8 16.8 %all-to-all-done.10 = bf16[16,256,48]{1,2,0:T(8,128)(2,1)S(1)} async-done(((bf16[16,256,48]{1,2,0:T(8,128)(2,1)}), bf16[16,256,48]{1,2,0:T(8,128)(2,1)S(1)}, u32[]{:S(2)}, u32[]{:S(2)}) %all-to-all-start.10) | async-done | bytes 393248 | tf_op jit(solution)/shard_map/all_to_all | solution.py:28
  260.0 17.6 %all_to_all.66 = bf16[32,8,96]{2,1,0:T(8,128)(2,1)S(1)} all-to-all(bf16[32,8,96]{2,1,0:T(8,128)(2,1)S(1)} %bitcast.176), channel_id=1, replica_groups=mesh['seq'=32,'mp'=16] {'seq'}, dimensions={0} | all-to-all | bytes 98304 | tf_op jit(solution)/shard_map/all_to_all | solution.py:24
  (179 shorter events, 54.9 us)
Async XLA Ops:
  0.0 219.6 %copy-start = (bf16[1,2,48,1536]{3,2,1,0:T(8,128)(2,1)S(1)}, bf16[1,2,48,1536]{3,2,1,0:T(8,128)(2,1)}, u32[]{:S(2)}) copy-start(bf16[1,2,48,1536]{3,2,1,0:T(8,128)(2,1)} %param.32) | copy-start | bytes 884740
  4.4 14.8 %copy-start.1 = (bf16[2,16,64,256]{3,2,1,0:T(8,128)(2,1)S(1)}, bf16[2,16,64,256]{3,2,1,0:T(8,128)(2,1)}, u32[]{:S(2)}) copy-start(bf16[2,16,64,256]{3,2,1,0:T(8,128)(2,1)} %param.26) | copy-start | bytes 3145732
  8.6 10.7 %copy-start.7 = (bf16[2,2,64,256]{3,2,1,0:T(8,128)(2,1)S(1)}, bf16[2,2,64,256]{3,2,1,0:T(8,128)(2,1)}, u32[]{:S(2)}) copy-start(bf16[2,2,64,256]{3,2,1,0:T(8,128)(2,1)} %param.25) | copy-start | bytes 393220
  8.6 19.6 %all-to-all-start = ((bf16[32,32,96]{2,1,0:T(8,128)(2,1)}), bf16[32,32,96]{2,1,0:T(8,128)(2,1)S(1)}, u32[]{:S(2)}, u32[]{:S(2)}) async-start(bf16[32,32,96]{2,1,0:T(8,128)(2,1)} %select_select_fusion), calls=%async_computation | async-start | bytes 524288 | tf_op jit(solution)/shard_map/all_to_all | solution.py:24
  29.0 24.3 %all-to-all-start.1 = ((f32[16,1,32]{2,1,0:T(1,128)}), f32[16,1,32]{2,1,0:T(1,128)S(1)}, u32[]{:S(2)}, u32[]{:S(2)}) async-start(f32[16,1,32]{2,1,0:T(1,128)} %broadcast_in_dim.248), calls=%async_computation.1 | async-start | bytes 16384 | tf_op jit(solution)/shard_map/all_to_all | solution.py:28
  43.6 9.7 %copy-start.16 = (f32[96]{0:T(128)S(1)}, f32[96]{0:T(128)}, u32[]{:S(2)}) copy-start(f32[96]{0:T(128)} %param.22) | copy-start | bytes 1156
  43.6 15.8 %copy-start.15 = (s32[2]{0:T(128)S(1)}, s32[2]{0:T(128)}, u32[]{:S(2)}) copy-start(s32[2]{0:T(128)} %param.28) | copy-start | bytes 28
  43.6 24.8 %copy-start.11 = (bf16[96,64]{0,1:T(8,128)(2,1)S(1)}, bf16[96,64]{0,1:T(8,128)(2,1)}, u32[]{:S(2)}) copy-start(bf16[96,64]{0,1:T(8,128)(2,1)} %param.23) | copy-start | bytes 36868
  54.1 19.1 %copy-start.18 = (s32[16]{0:T(128)S(1)}, s32[16]{0:T(128)}, u32[]{:S(2)}) copy-start(s32[16]{0:T(128)} %param.27) | copy-start | bytes 196
  54.1 20.5 %copy-start.19 = (s32[16]{0:T(128)S(1)}, s32[16]{0:T(128)}, u32[]{:S(2)}) copy-start(s32[16]{0:T(128)} %param.29) | copy-start | bytes 196
  54.1 20.6 %copy-start.17 = (s32[64]{0:T(128)S(1)}, s32[64]{0:T(128)}, u32[]{:S(2)}) copy-start(s32[64]{0:T(128)} %constant.114) | copy-start | bytes 772
  54.1 14.3 %all-to-all-start.2 = ((bf16[32,32,96]{2,1,0:T(8,128)(2,1)}), bf16[32,32,96]{2,1,0:T(8,128)(2,1)S(1)}, u32[]{:S(2)}, u32[]{:S(2)}) async-start(bf16[32,32,96]{2,1,0:T(8,128)(2,1)} %broadcast_in_dim.249), calls=%async_computation.2 | async-start | bytes 524288 | tf_op jit(solution)/shard_map/all_to_all | solution.py:28
  69.7 18.0 %all-to-all-start.3 = ((f32[16,1,4096]{2,1,0:T(1,128)}), f32[16,1,4096]{2,1,0:T(1,128)S(1)}, u32[]{:S(2)}, u32[]{:S(2)}) async-start(f32[16,1,4096]{2,1,0:T(1,128)} %reshape.353), calls=%async_computation.3 | async-start | bytes 524288 | tf_op jit(solution)/shard_map/all_to_all | solution.py:24
  89.7 9.5 %copy-start.5 = (bf16[64,2,128]{2,0,1:T(8,128)(2,1)S(1)}, bf16[64,2,128]{2,0,1:T(8,128)(2,1)}, u32[]{:S(2)}) copy-start(bf16[64,2,128]{2,0,1:T(8,128)(2,1)} %copy.241) | copy-start | bytes 98308
  90.9 17.3 %all-to-all-start.4 = ((bf16[32,2,2048]{2,1,0:T(2,128)(2,1)}), bf16[32,2,2048]{2,1,0:T(2,128)(2,1)S(1)}, u32[]{:S(2)}, u32[]{:S(2)}) async-start(bf16[32,2,2048]{2,1,0:T(2,128)(2,1)} %reshape.355), calls=%async_computation.4 | async-start | bytes 524288 | tf_op jit(solution)/shard_map/all_to_all | solution.py:28
  121.8 14.6 %all-to-all-start.5 = ((f32[32,1,3328]{2,1,0:T(1,128)}), f32[32,1,3328]{2,1,0:T(1,128)S(1)}, u32[]{:S(2)}, u32[]{:S(2)}) async-start(f32[32,1,3328]{2,1,0:T(1,128)} %reshape.357), calls=%async_computation.5 | async-start | bytes 851968 | tf_op jit(solution)/shard_map/all_to_all | solution.py:24
  139.2 19.1 %copy-start.13 = (bf16[48,96]{1,0:T(8,128)(2,1)S(1)}, bf16[48,96]{1,0:T(8,128)(2,1)}, u32[]{:S(2)}) copy-start(bf16[48,96]{1,0:T(8,128)(2,1)} %param.24) | copy-start | bytes 27652
  140.0 17.9 %all-to-all-start.6 = ((bf16[16,2,1536]{2,1,0:T(2,128)(2,1)}), bf16[16,2,1536]{2,1,0:T(2,128)(2,1)S(1)}, u32[]{:S(2)}, u32[]{:S(2)}) async-start(bf16[16,2,1536]{2,1,0:T(2,128)(2,1)} %reshape.359), calls=%async_computation.6 | async-start | bytes 196608 | tf_op jit(solution)/shard_map/all_to_all | solution.py:28
  159.3 16.9 %all-to-all-start.7 = ((f32[32,32,96]{2,1,0:T(8,128)}), f32[32,32,96]{2,1,0:T(8,128)S(1)}, u32[]{:S(2)}, u32[]{:S(2)}) async-start(f32[32,32,96]{2,1,0:T(8,128)} %fusion.60), calls=%async_computation.7 | async-start | bytes 1048576 | tf_op jit(solution)/shard_map/all_to_all | solution.py:24
  177.0 16.5 %all-to-all-start.8 = ((bf16[16,32,96]{2,1,0:T(8,128)(2,1)}), bf16[16,32,96]{2,1,0:T(8,128)(2,1)S(1)}, u32[]{:S(2)}, u32[]{:S(2)}) async-start(bf16[16,32,96]{2,1,0:T(8,128)(2,1)} %broadcast_in_dim.267), calls=%async_computation.8 | async-start | bytes 262144 | tf_op jit(solution)/shard_map/all_to_all | solution.py:28
  195.1 20.2 %all-to-all-start.9 = ((bf16[32,8,1536]{2,1,0:T(8,128)(2,1)}), bf16[32,8,1536]{2,1,0:T(8,128)(2,1)S(1)}, u32[]{:S(2)}, u32[]{:S(2)}) async-start(bf16[32,8,1536]{2,1,0:T(8,128)(2,1)} %convolution_convert_fusion), calls=%async_computation.9 | async-start | bytes 1572864 | tf_op jit(solution)/shard_map/all_to_all | solution.py:24
  215.4 17.5 %all-to-all-start.11 = ((bf16[16,48,96]{2,1,0:T(8,128)(2,1)}), bf16[16,48,96]{2,1,0:T(8,128)(2,1)S(1)}, u32[]{:S(2)}, u32[]{:S(2)}) async-start(bf16[16,48,96]{2,1,0:T(8,128)(2,1)} %bitcast.161), calls=%async_computation.11 | async-start | bytes 393216 | tf_op jit(solution)/shard_map/all_to_all | solution.py:24
  220.0 22.4 %copy-start.9 = (bf16[1536,32]{0,1:T(8,128)(2,1)S(1)}, bf16[1536,32]{0,1:T(8,128)(2,1)}, u32[]{:S(2)}) copy-start(bf16[1536,32]{0,1:T(8,128)(2,1)} %param.31) | copy-start | bytes 294916
  233.6 26.0 %all-to-all-start.10 = ((bf16[16,256,48]{1,2,0:T(8,128)(2,1)}), bf16[16,256,48]{1,2,0:T(8,128)(2,1)S(1)}, u32[]{:S(2)}, u32[]{:S(2)}) async-start(bf16[16,256,48]{1,2,0:T(8,128)(2,1)} %broadcast_in_dim.268), calls=%async_computation.10 | async-start | bytes 786432 | tf_op jit(solution)/shard_map/all_to_all | solution.py:28
  (8 other events, 48.3 us)

commit v4 on v3

--- a/solution.py
+++ b/solution.py
@@ -60,7 +60,12 @@
     got = exchange(looked.reshape(n_seq, home_rows, feat_mp), "seq")
     x_home = jnp.sum(got.astype(jnp.float32), axis=0)
 
-    square_sum = jnp.sum(gather_by_exchange(jnp.sum(x_home * x_home, axis=-1), "mp", n_mp), axis=0)
+    half = w_down.shape[1]
+    down_send = w_down[0].reshape(half, n_mp, feat_mp).transpose(1, 0, 2).reshape(n_mp, half * feat_mp)
+    own_squares = jnp.broadcast_to(jnp.sum(x_home * x_home, axis=-1)[None], (n_mp, home_rows))
+    mp_got = exchange(jnp.concatenate([own_squares, down_send.astype(jnp.float32)], axis=1), "mp")
+    square_sum = jnp.sum(mp_got[:, :home_rows], axis=0)
+    down_cols = mp_got[:, home_rows:].astype(jnp.bfloat16).reshape(n_mp * half, feat_mp)
     normed = (x_home * lax.rsqrt(square_sum[:, None] / D + EPS) * attn_gain).astype(jnp.bfloat16)
     normed_all = gather_by_exchange(normed, "seq", n_seq).reshape(total_rows, feat_mp)
 
@@ -187,8 +192,6 @@
     hidden = (jnp.maximum(both[:, :half], 0.0) * both[:, half:]).astype(jnp.bfloat16)
     hidden_all = gather_by_exchange(hidden, "mp", n_mp)
     hidden_all = hidden_all.transpose(1, 0, 2).reshape(n_seq * MOST, n_mp * half)
-    down_cols = exchange(w_down[0].reshape(half, n_mp, feat_mp).transpose(1, 0, 2), "mp")
-    down_cols = down_cols.reshape(n_mp * half, feat_mp)
     expert_out = jnp.dot(hidden_all, down_cols, preferred_element_type=jnp.float32).astype(jnp.bfloat16)
     weighted = (share[:, None] * expert_out.astype(jnp.float32)).astype(jnp.bfloat16)
     back = exchange(weighted.reshape(n_seq, MOST, feat_mp), "seq")

time: 280 us -> 269 us (0.961)
  waiting for transfers between devices: 131 us -> 106 us
  blocking collectives: 17.6 us -> 36.8 us
  starting transfers between devices: 77.7 us -> 70.2 us
  other arithmetic: 12.6 us -> 15.6 us
    all_to_all x1 -> x2, blocking collectives: 17.6 us -> 36.8 us  [exchange(): return lax.all_to_all(values, axis, 0, 0, tiled=True)]
    all_to_all x6 -> x5, waiting for transfers between devices: 63.9 us -> 48.4 us  [exchange(): return lax.all_to_all(values, axis, 0, 0, tiled=True)]
    all_to_all x6 -> x5, starting transfers between devices: 44.2 us -> 32 us  [gather_by_exchange(): lax.all_to_all(jnp.broadcast_to(values[None], (n,) + values.shape), axis,...]
    all_to_all x6 -> x5, waiting for transfers between devices: 66.9 us -> 57.3 us  [gather_by_exchange(): lax.all_to_all(jnp.broadcast_to(values[None], (n,) + values.shape), axis,...]
    all_to_all x6 -> x5, starting transfers between devices: 33.5 us -> 38.2 us  [exchange(): return lax.all_to_all(values, axis, 0, 0, tiled=True)]
    unnamed x52 -> x53, local copies, waits for them, and re-layouts: 7.8 us -> 8.55 us
  transfers between devices with their start and end apart: 12 -> 10, of which waited for: 12 -> 10; matrix products, arithmetic and copies ran while one was open for 5% -> 6% of each run, Pallas kernels for 0% -> 0%
where the time goes in v4:
time: 269 us; the launch traced here: 268 us
  waiting for transfers between devices  106 us (39%)
  starting transfers between devices  70.2 us (26%)
  blocking collectives  36.8 us (14%)
  local copies, waits for them, and re-layouts  31.1 us (12%)
  other arithmetic  15.6 us (6%)
  matrix products  7.54 us (3%)
    all_to_all x5, waiting for transfers between devices, gather_by_exchange(): lax.all_to_all(jnp.broadcast_to(values[None], (n,) + values.shape), axis,...  57.3 us
    all_to_all x5, waiting for transfers between devices, exchange(): return lax.all_to_all(values, axis, 0, 0, tiled=True)  48.4 us
    all_to_all x5, starting transfers between devices, exchange(): return lax.all_to_all(values, axis, 0, 0, tiled=True)  38.2 us
    all_to_all x2, blocking collectives, exchange(): return lax.all_to_all(values, axis, 0, 0, tiled=True)  36.8 us
    all_to_all x5, starting transfers between devices, gather_by_exchange(): lax.all_to_all(jnp.broadcast_to(values[None], (n,) + values.shape), axis,...  32 us
    unnamed x53, local copies, waits for them, and re-layouts  8.55 us
  transfers between devices with their start and end apart: 10, of which 10 were waited for; matrix products, arithmetic and copies ran while one was open for 6% of the time, Pallas kernels for 0%

profile of v4, /device:TPU:1, one launch (start us, length us, event | category | flops | bytes accessed | tf_op | source)
XLA Modules:
  0.0 268.0 jit_solution(4834749512117948522)
XLA Ops:
  2.2 2.2 copy.188
  4.4 3.2 %gather_fusion = bf16[1024,96]{1,0:T(8,128)(2,1)S(1)} fusion(bf16[4748,96]{1,0:T(8,128)(2,1)S(1)} %copy.188, s32[1024]{0:T(1024)S(1)} %broadcast_clamp_fusion), kind=kCustom, calls=%fused_computation.2 | custom fusion | bytes 397312 | tf_op jit(solution)/shard_map/jit(_take)/gather | solution.py:58
  8.6 10.4 %all-to-all-start = ((bf16[32,32,96]{2,1,0:T(8,128)(2,1)}), bf16[32,32,96]{2,1,0:T(8,128)(2,1)S(1)}, u32[]{:S(2)}, u32[]{:S(2)}) async-start(bf16[32,32,96]{2,1,0:T(8,128)(2,1)} %select_select_fusion), calls=%async_computation | async-start | bytes 524288 | tf_op jit(solution)/shard_map/all_to_all | solution.py:24
  19.5 8.6 %all-to-all-done = bf16[32,32,96]{2,1,0:T(8,128)(2,1)S(1)} async-done(((bf16[32,32,96]{2,1,0:T(8,128)(2,1)}), bf16[32,32,96]{2,1,0:T(8,128)(2,1)S(1)}, u32[]{:S(2)}, u32[]{:S(2)}) %all-to-all-start) | async-done | bytes 196640 | tf_op jit(solution)/shard_map/all_to_all | solution.py:24
  29.4 13.0 %all-to-all-start.1 = ((f32[16,1,4640]{2,1,0:T(1,128)}), f32[16,1,4640]{2,1,0:T(1,128)S(1)}, u32[]{:S(2)}, u32[]{:S(2)}) async-start(f32[16,1,4640]{2,1,0:T(1,128)} %copy.196), calls=%async_computation.1 | async-start | bytes 606208 | tf_op jit(solution)/shard_map/all_to_all | solution.py:24
  45.0 11.9 %all-to-all-done.1 = f32[16,1,4640]{2,1,0:T(1,128)S(1)} async-done(((f32[16,1,4640]{2,1,0:T(1,128)}), f32[16,1,4640]{2,1,0:T(1,128)S(1)}, u32[]{:S(2)}, u32[]{:S(2)}) %all-to-all-start.1) | async-done | bytes 296992 | tf_op jit(solution)/shard_map/all_to_all | solution.py:24
  58.5 10.1 %all-to-all-start.2 = ((bf16[32,32,96]{2,1,0:T(8,128)(2,1)}), bf16[32,32,96]{2,1,0:T(8,128)(2,1)S(1)}, u32[]{:S(2)}, u32[]{:S(2)}) async-start(bf16[32,32,96]{2,1,0:T(8,128)(2,1)} %broadcast_in_dim.249), calls=%async_computation.2 | async-start | bytes 524288 | tf_op jit(solution)/shard_map/all_to_all | solution.py:28
  69.2 8.5 %all-to-all-done.2 = bf16[32,32,96]{2,1,0:T(8,128)(2,1)S(1)} async-done(((bf16[32,32,96]{2,1,0:T(8,128)(2,1)}), bf16[32,32,96]{2,1,0:T(8,128)(2,1)S(1)}, u32[]{:S(2)}, u32[]{:S(2)}) %all-to-all-start.2) | async-done | bytes 196640 | tf_op jit(solution)/shard_map/all_to_all | solution.py:28
  78.9 5.7 %all-to-all-start.3 = ((f32[16,1,4096]{2,1,0:T(1,128)}), f32[16,1,4096]{2,1,0:T(1,128)S(1)}, u32[]{:S(2)}, u32[]{:S(2)}) async-start(f32[16,1,4096]{2,1,0:T(1,128)} %reshape.363), calls=%async_computation.3 | async-start | bytes 524288 | tf_op jit(solution)/shard_map/all_to_all | solution.py:24
  86.7 12.1 %all-to-all-done.3 = f32[16,1,4096]{2,1,0:T(1,128)S(1)} async-done(((f32[16,1,4096]{2,1,0:T(1,128)}), f32[16,1,4096]{2,1,0:T(1,128)S(1)}, u32[]{:S(2)}, u32[]{:S(2)}) %all-to-all-start.3) | async-done | bytes 262176 | tf_op jit(solution)/shard_map/all_to_all | solution.py:24
  102.0 8.5 %all-to-all-start.4 = ((bf16[32,2,2048]{2,1,0:T(2,128)(2,1)}), bf16[32,2,2048]{2,1,0:T(2,128)(2,1)S(1)}, u32[]{:S(2)}, u32[]{:S(2)}) async-start(bf16[32,2,2048]{2,1,0:T(2,128)(2,1)} %reshape.365), calls=%async_computation.4 | async-start | bytes 524288 | tf_op jit(solution)/shard_map/all_to_all | solution.py:28
  111.5 8.1 %all-to-all-done.4 = bf16[32,2,2048]{2,1,0:T(2,128)(2,1)S(1)} async-done(((bf16[32,2,2048]{2,1,0:T(2,128)(2,1)}), bf16[32,2,2048]{2,1,0:T(2,128)(2,1)S(1)}, u32[]{:S(2)}, u32[]{:S(2)}) %all-to-all-start.4) | async-done | bytes 262176 | tf_op jit(solution)/shard_map/all_to_all | solution.py:28
  133.2 3.7 %all-to-all-start.5 = ((f32[32,1,3328]{2,1,0:T(1,128)}), f32[32,1,3328]{2,1,0:T(1,128)S(1)}, u32[]{:S(2)}, u32[]{:S(2)}) async-start(f32[32,1,3328]{2,1,0:T(1,128)} %reshape.367), calls=%async_computation.5 | async-start | bytes 851968 | tf_op jit(solution)/shard_map/all_to_all | solution.py:24
  141.5 6.2 %all-to-all-done.5 = f32[32,1,3328]{2,1,0:T(1,128)S(1)} async-done(((f32[32,1,3328]{2,1,0:T(1,128)}), f32[32,1,3328]{2,1,0:T(1,128)S(1)}, u32[]{:S(2)}, u32[]{:S(2)}) %all-to-all-start.5) | async-done | bytes 426016 | tf_op jit(solution)/shard_map/all_to_all | solution.py:24
  151.2 5.7 %all-to-all-start.6 = ((bf16[16,2,1536]{2,1,0:T(2,128)(2,1)}), bf16[16,2,1536]{2,1,0:T(2,128)(2,1)S(1)}, u32[]{:S(2)}, u32[]{:S(2)}) async-start(bf16[16,2,1536]{2,1,0:T(2,128)(2,1)} %reshape.369), calls=%async_computation.6 | async-start | bytes 196608 | tf_op jit(solution)/shard_map/all_to_all | solution.py:28
  157.5 11.7 %all-to-all-done.6 = bf16[16,2,1536]{2,1,0:T(2,128)(2,1)S(1)} async-done(((bf16[16,2,1536]{2,1,0:T(2,128)(2,1)}), bf16[16,2,1536]{2,1,0:T(2,128)(2,1)S(1)}, u32[]{:S(2)}, u32[]{:S(2)}) %all-to-all-start.6) | async-done | bytes 98336 | tf_op jit(solution)/shard_map/all_to_all | solution.py:28
  170.5 5.4 %all-to-all-start.7 = ((f32[32,32,96]{2,1,0:T(8,128)}), f32[32,32,96]{2,1,0:T(8,128)S(1)}, u32[]{:S(2)}, u32[]{:S(2)}) async-start(f32[32,32,96]{2,1,0:T(8,128)} %fusion.58), calls=%async_computation.7 | async-start | bytes 1048576 | tf_op jit(solution)/shard_map/all_to_all | solution.py:24
  177.8 9.7 %all-to-all-done.7 = f32[32,32,96]{2,1,0:T(8,128)S(1)} async-done(((f32[32,32,96]{2,1,0:T(8,128)}), f32[32,32,96]{2,1,0:T(8,128)S(1)}, u32[]{:S(2)}, u32[]{:S(2)}) %all-to-all-start.7) | async-done | bytes 393248 | tf_op jit(solution)/shard_map/all_to_all | solution.py:24
  188.2 3.8 %all-to-all-start.8 = ((bf16[16,32,96]{2,1,0:T(8,128)(2,1)}), bf16[16,32,96]{2,1,0:T(8,128)(2,1)S(1)}, u32[]{:S(2)}, u32[]{:S(2)}) async-start(bf16[16,32,96]{2,1,0:T(8,128)(2,1)} %broadcast_in_dim.267), calls=%async_computation.8 | async-start | bytes 262144 | tf_op jit(solution)/shard_map/all_to_all | solution.py:28
  192.9 11.7 %all-to-all-done.8 = bf16[16,32,96]{2,1,0:T(8,128)(2,1)S(1)} async-done(((bf16[16,32,96]{2,1,0:T(8,128)(2,1)}), bf16[16,32,96]{2,1,0:T(8,128)(2,1)S(1)}, u32[]{:S(2)}, u32[]{:S(2)}) %all-to-all-start.8) | async-done | bytes 98336 | tf_op jit(solution)/shard_map/all_to_all | solution.py:28
  205.5 20.0 %all_to_all.67 = bf16[32,8,1536]{2,1,0:T(8,128)(2,1)S(1)} all-to-all(bf16[32,8,1536]{2,1,0:T(8,128)(2,1)S(1)} %convolution_convert_fusion), channel_id=1, replica_groups=mesh['seq'=32,'mp'=16] {'seq'}, dimensions={0} | all-to-all | bytes 1572864 | tf_op jit(solution)/shard_map/all_to_all | solution.py:24
  226.7 3.9 %all-to-all-start.10 = ((bf16[16,256,48]{1,2,0:T(8,128)(2,1)}), bf16[16,256,48]{1,2,0:T(8,128)(2,1)S(1)}, u32[]{:S(2)}, u32[]{:S(2)}) async-start(bf16[16,256,48]{1,2,0:T(8,128)(2,1)} %broadcast_in_dim.268), calls=%async_computation.10 | async-start | bytes 786432 | tf_op jit(solution)/shard_map/all_to_all | solution.py:28
  232.7 17.3 %all-to-all-done.10 = bf16[16,256,48]{1,2,0:T(8,128)(2,1)S(1)} async-done(((bf16[16,256,48]{1,2,0:T(8,128)(2,1)}), bf16[16,256,48]{1,2,0:T(8,128)(2,1)S(1)}, u32[]{:S(2)}, u32[]{:S(2)}) %all-to-all-start.10) | async-done | bytes 393248 | tf_op jit(solution)/shard_map/all_to_all | solution.py:28
  250.4 16.8 %all_to_all.68 = bf16[32,8,96]{2,1,0:T(8,128)(2,1)S(1)} all-to-all(bf16[32,8,96]{2,1,0:T(8,128)(2,1)S(1)} %bitcast.175), channel_id=1, replica_groups=mesh['seq'=32,'mp'=16] {'seq'}, dimensions={0} | all-to-all | bytes 98304 | tf_op jit(solution)/shard_map/all_to_all | solution.py:24
  (182 shorter events, 48.9 us)
Async XLA Ops:
  0.0 225.5 %copy-start = (bf16[1,2,48,1536]{3,2,1,0:T(8,128)(2,1)S(1)}, bf16[1,2,48,1536]{3,2,1,0:T(8,128)(2,1)}, u32[]{:S(2)}) copy-start(bf16[1,2,48,1536]{3,2,1,0:T(8,128)(2,1)} %param.32) | copy-start | bytes 884740
  4.4 14.6 %copy-start.5 = (bf16[1,48,1536]{2,1,0:T(8,128)(2,1)S(1)}, bf16[1,48,1536]{2,1,0:T(8,128)(2,1)}, u32[]{:S(2)}) copy-start(bf16[1,48,1536]{2,1,0:T(8,128)(2,1)} %param.33) | copy-start | bytes 442372
  8.6 19.4 %all-to-all-start = ((bf16[32,32,96]{2,1,0:T(8,128)(2,1)}), bf16[32,32,96]{2,1,0:T(8,128)(2,1)S(1)}, u32[]{:S(2)}, u32[]{:S(2)}) async-start(bf16[32,32,96]{2,1,0:T(8,128)(2,1)} %select_select_fusion), calls=%async_computation | async-start | bytes 524288 | tf_op jit(solution)/shard_map/all_to_all | solution.py:24
  19.5 23.0 %copy-start.6 = (bf16[2,2,64,256]{3,2,1,0:T(8,128)(2,1)S(1)}, bf16[2,2,64,256]{3,2,1,0:T(8,128)(2,1)}, u32[]{:S(2)}) copy-start(bf16[2,2,64,256]{3,2,1,0:T(8,128)(2,1)} %param.25) | copy-start | bytes 393220
  28.3 14.4 %copy-start.1 = (bf16[2,16,64,256]{3,2,1,0:T(8,128)(2,1)S(1)}, bf16[2,16,64,256]{3,2,1,0:T(8,128)(2,1)}, u32[]{:S(2)}) copy-start(bf16[2,16,64,256]{3,2,1,0:T(8,128)(2,1)} %param.26) | copy-start | bytes 3145732
  29.4 27.5 %all-to-all-start.1 = ((f32[16,1,4640]{2,1,0:T(1,128)}), f32[16,1,4640]{2,1,0:T(1,128)S(1)}, u32[]{:S(2)}, u32[]{:S(2)}) async-start(f32[16,1,4640]{2,1,0:T(1,128)} %copy.196), calls=%async_computation.1 | async-start | bytes 606208 | tf_op jit(solution)/shard_map/all_to_all | solution.py:24
  43.0 14.7 %copy-start.16 = (f32[96]{0:T(128)S(1)}, f32[96]{0:T(128)}, u32[]{:S(2)}) copy-start(f32[96]{0:T(128)} %param.22) | copy-start | bytes 1156
  43.1 25.5 %copy-start.15 = (s32[2]{0:T(128)S(1)}, s32[2]{0:T(128)}, u32[]{:S(2)}) copy-start(s32[2]{0:T(128)} %param.28) | copy-start | bytes 28
  43.1 34.5 %copy-start.8 = (bf16[96,64]{0,1:T(8,128)(2,1)S(1)}, bf16[96,64]{0,1:T(8,128)(2,1)}, u32[]{:S(2)}) copy-start(bf16[96,64]{0,1:T(8,128)(2,1)} %param.23) | copy-start | bytes 36868
  58.5 26.1 %copy-start.18 = (s32[16]{0:T(128)S(1)}, s32[16]{0:T(128)}, u32[]{:S(2)}) copy-start(s32[16]{0:T(128)} %param.27) | copy-start | bytes 196
  58.5 27.3 %copy-start.19 = (s32[16]{0:T(128)S(1)}, s32[16]{0:T(128)}, u32[]{:S(2)}) copy-start(s32[16]{0:T(128)} %param.29) | copy-start | bytes 196
  58.5 28.1 %copy-start.17 = (s32[64]{0:T(128)S(1)}, s32[64]{0:T(128)}, u32[]{:S(2)}) copy-start(s32[64]{0:T(128)} %constant.114) | copy-start | bytes 772
  58.5 19.1 %all-to-all-start.2 = ((bf16[32,32,96]{2,1,0:T(8,128)(2,1)}), bf16[32,32,96]{2,1,0:T(8,128)(2,1)S(1)}, u32[]{:S(2)}, u32[]{:S(2)}) async-start(bf16[32,32,96]{2,1,0:T(8,128)(2,1)} %broadcast_in_dim.249), calls=%async_computation.2 | async-start | bytes 524288 | tf_op jit(solution)/shard_map/all_to_all | solution.py:28
  78.9 19.8 %all-to-all-start.3 = ((f32[16,1,4096]{2,1,0:T(1,128)}), f32[16,1,4096]{2,1,0:T(1,128)S(1)}, u32[]{:S(2)}, u32[]{:S(2)}) async-start(f32[16,1,4096]{2,1,0:T(1,128)} %reshape.363), calls=%async_computation.3 | async-start | bytes 524288 | tf_op jit(solution)/shard_map/all_to_all | solution.py:24
  102.0 17.6 %all-to-all-start.4 = ((bf16[32,2,2048]{2,1,0:T(2,128)(2,1)}), bf16[32,2,2048]{2,1,0:T(2,128)(2,1)S(1)}, u32[]{:S(2)}, u32[]{:S(2)}) async-start(bf16[32,2,2048]{2,1,0:T(2,128)(2,1)} %reshape.365), calls=%async_computation.4 | async-start | bytes 524288 | tf_op jit(solution)/shard_map/all_to_all | solution.py:28
  133.2 14.4 %all-to-all-start.5 = ((f32[32,1,3328]{2,1,0:T(1,128)}), f32[32,1,3328]{2,1,0:T(1,128)S(1)}, u32[]{:S(2)}, u32[]{:S(2)}) async-start(f32[32,1,3328]{2,1,0:T(1,128)} %reshape.367), calls=%async_computation.5 | async-start | bytes 851968 | tf_op jit(solution)/shard_map/all_to_all | solution.py:24
  141.3 8.3 %copy-start.13 = (pred[48]{0:T(512)(128)(4,1)S(1)}, pred[48]{0:T(512)(128)(4,1)}, u32[]{:S(2)}) copy-start(pred[48]{0:T(512)(128)(4,1)} %subtract_compare_fusion) | copy-start | bytes 148
  141.4 8.4 %copy-start.12 = (pred[48]{0:T(512)(128)(4,1)S(1)}, pred[48]{0:T(512)(128)(4,1)}, u32[]{:S(2)}) copy-start(pred[48]{0:T(512)(128)(4,1)} %compare_and_fusion.2) | copy-start | bytes 148
  149.5 7.4 %copy-start.9 = (s32[256,4,4]{0,2,1:T(4,128)S(1)}, s32[256,4,4]{0,2,1:T(4,128)}, u32[]{:S(2)}) copy-start(s32[256,4,4]{0,2,1:T(4,128)} %param.34) | copy-start | bytes 49156
  150.4 19.2 %copy-start.10 = (bf16[48,96]{1,0:T(8,128)(2,1)S(1)}, bf16[48,96]{1,0:T(8,128)(2,1)}, u32[]{:S(2)}) copy-start(bf16[48,96]{1,0:T(8,128)(2,1)} %param.24) | copy-start | bytes 27652
  151.2 18.0 %all-to-all-start.6 = ((bf16[16,2,1536]{2,1,0:T(2,128)(2,1)}), bf16[16,2,1536]{2,1,0:T(2,128)(2,1)S(1)}, u32[]{:S(2)}, u32[]{:S(2)}) async-start(bf16[16,2,1536]{2,1,0:T(2,128)(2,1)} %reshape.369), calls=%async_computation.6 | async-start | bytes 196608 | tf_op jit(solution)/shard_map/all_to_all | solution.py:28
  170.5 17.0 %all-to-all-start.7 = ((f32[32,32,96]{2,1,0:T(8,128)}), f32[32,32,96]{2,1,0:T(8,128)S(1)}, u32[]{:S(2)}, u32[]{:S(2)}) async-start(f32[32,32,96]{2,1,0:T(8,128)} %fusion.58), calls=%async_computation.7 | async-start | bytes 1048576 | tf_op jit(solution)/shard_map/all_to_all | solution.py:24
  188.2 16.4 %all-to-all-start.8 = ((bf16[16,32,96]{2,1,0:T(8,128)(2,1)}), bf16[16,32,96]{2,1,0:T(8,128)(2,1)S(1)}, u32[]{:S(2)}, u32[]{:S(2)}) async-start(bf16[16,32,96]{2,1,0:T(8,128)(2,1)} %broadcast_in_dim.267), calls=%async_computation.8 | async-start | bytes 262144 | tf_op jit(solution)/shard_map/all_to_all | solution.py:28
  226.7 23.3 %all-to-all-start.10 = ((bf16[16,256,48]{1,2,0:T(8,128)(2,1)}), bf16[16,256,48]{1,2,0:T(8,128)(2,1)S(1)}, u32[]{:S(2)}, u32[]{:S(2)}) async-start(bf16[16,256,48]{1,2,0:T(8,128)(2,1)} %broadcast_in_dim.268), calls=%async_computation.10 | async-start | bytes 786432 | tf_op jit(solution)/shard_map/all_to_all | solution.py:28
  (6 other events, 26.5 us)
